TPU v7x, 32 devices: a whole 2x2x4 slice. The times are simulated.
32 devices in a mesh: dp: 8 (over y, x, core), tensor: 4 (over z).
Axes of the slice: x: 2, y: 2, z: 4, core: 2. Of those that a mesh axis runs over, the one named last changes fastest.
Arguments:
- inputs: bfloat16 [16384, 768], P(('dp', 'tensor')), may hold values from -6 to 6
- prefix: int32 [16], P('dp'), may hold values from 102 to 512, as said below
- cotangent: bfloat16 [16384, 768], P(('dp', 'tensor')), may hold values from -6 to 6
- w_query: bfloat16 [768, 768], P('dp', 'tensor'), may hold values from -0.3125 to 0.3125
- w_key: bfloat16 [768, 768], P('dp', 'tensor'), may hold values from -0.3125 to 0.3125
- w_value: bfloat16 [768, 768], P('dp', 'tensor'), may hold values from -0.21875 to 0.21875
- w_out: bfloat16 [768, 768], P('tensor', 'dp'), may hold values from -0.875 to 0.875
- w_up: bfloat16 [768, 3072], P('dp', 'tensor'), may hold values from -0.21875 to 0.21875
- w_down: bfloat16 [3072, 768], P('tensor', 'dp'), may hold values from -0.109375 to 0.109375
- b_query: bfloat16 [768], replicated, may hold values from -3 to 3
- b_value: bfloat16 [768], replicated, may hold values from -3 to 3
- b_out: bfloat16 [768], replicated, may hold values from -2 to 2
- b_up: bfloat16 [3072], replicated, may hold values from -3 to 3
- b_down: bfloat16 [768], replicated, may hold values from -2 to 2
- gain_one: bfloat16 [768], replicated, may hold values from 0.25 to 1.75
- shift_one: bfloat16 [768], replicated, may hold values from -2 to 2
- gain_two: bfloat16 [768], replicated, may hold values from 0.25 to 1.75
- shift_two: bfloat16 [768], replicated, may hold values from -2 to 2
Outputs:
- output: bfloat16 [16384, 768], P(('dp', 'tensor'))
- grad_input: float32 [16384, 768], P(('dp', 'tensor'))
- grad_w_query: float32 [768, 768], P('dp', 'tensor')
- grad_w_key: float32 [768, 768], P('dp', 'tensor')
- grad_w_value: float32 [768, 768], P('dp', 'tensor')
- grad_w_out: float32 [768, 768], P('tensor', 'dp')
- grad_w_up: float32 [768, 3072], P('dp', 'tensor')
- grad_w_down: float32 [3072, 768], P('tensor', 'dp')
- grad_b_query: float32 [768], replicated
- grad_b_value: float32 [768], replicated
- grad_b_out: float32 [768], replicated
- grad_b_up: float32 [3072], replicated
- grad_b_down: float32 [768], replicated
- grad_gain_one: float32 [768], replicated
- grad_shift_one: float32 [768], replicated
- grad_gain_two: float32 [768], replicated
- grad_shift_two: float32 [768], replicated
Inputs may be any that keep to these rules, and one draw needn't show every extreme that they name: Every draw has a sequence whose prefix is exactly 512.
All inputs are finite; a program needn't handle non-finite values.
Results may differ from a plain program's by a relative error of at most 0.015.
Values may be sent and summed in bfloat16 or wider, within the bound.
No kernel may reach another device: no remote copies, remote signals or barrier semaphores. Data moves between devices by JAX's collectives and lax.ppermute only.
A program may use at most 192 MiB of HBM per device.

v0:
```python
import jax
import jax.numpy as jnp
from jax import lax
from jax.sharding import PartitionSpec as P

HEAD = 64
SEQ_LEN = 1024


norm_eps = 1e-12
masked_score = -1e30


def layer_norm(values, norm_gain, norm_shift):
    center = values - jnp.mean(values, axis=-1, keepdims=True)
    spread = jnp.mean(center * center, axis=-1, keepdims=True)
    return center * lax.rsqrt(spread + norm_eps) * norm_gain + norm_shift


def gelu_exact(values):
    return jax.nn.gelu(values, approximate=False)


def dot_right(first_op, second_op):
    return jnp.dot(first_op, second_op, preferred_element_type=jnp.float32)


def dot_back(first_op, second_op):
    return lax.dot_general(
        first_op, second_op, (((1,), (1,)), ((), ())), preferred_element_type=jnp.float32
    )


def dot_over_rows(first_op, second_op):
    return lax.dot_general(
        first_op, second_op, (((0,), (0,)), ((), ())), preferred_element_type=jnp.float32
    )


def block_rows():
    return min(512, SEQ_LEN)


def key_stop(begin_row, block_size):
    prefix_end = -(-(SEQ_LEN // 2) // block_size) * block_size
    return min(SEQ_LEN, max(begin_row + block_size, prefix_end))


def block_scores(queries, key_rows, lengths, begin_row, block_size, stop_key):
    scaling = HEAD ** (-0.5)
    scores = (
        jnp.einsum(
            "sqhe,skhe->shqk",
            queries[:, begin_row : begin_row + block_size],
            key_rows[:, :stop_key],
            preferred_element_type=jnp.float32,
        )
        * scaling
    )
    row_index = begin_row + lax.broadcasted_iota(jnp.int32, (block_size, stop_key), 0)
    col_index = lax.broadcasted_iota(jnp.int32, (block_size, stop_key), 1)
    visible = (col_index <= row_index)[None, None] | (
        col_index[None, None] < lengths[:, None, None, None]
    )
    return jnp.where(visible, scores, masked_score)


def attend_forward(queries, key_rows, value_rows, lengths):
    block_size = block_rows()
    outputs = []
    log_sums = []
    for begin_row in range(0, SEQ_LEN, block_size):
        stop_key = key_stop(begin_row, block_size)
        scores = block_scores(queries, key_rows, lengths, begin_row, block_size, stop_key)
        row_top = jnp.max(scores, axis=-1, keepdims=True)
        exponent = jnp.exp(scores - row_top)
        row_total = jnp.sum(exponent, axis=-1, keepdims=True)
        probability = (exponent / row_total).astype(jnp.bfloat16)
        outputs.append(
            jnp.einsum(
                "shqk,skhe->sqhe",
                probability,
                value_rows[:, :stop_key],
                preferred_element_type=jnp.float32,
            )
        )
        log_sums.append(row_top[..., 0] + jnp.log(row_total[..., 0]))
    return (jnp.concatenate(outputs, axis=1), jnp.concatenate(log_sums, axis=2))


def attend_backward(queries, key_rows, value_rows, grad_attn, log_sums, lengths):
    block_size = block_rows()
    scaling = HEAD ** (-0.5)
    grad_queries = []
    grad_keys = jnp.zeros(key_rows.shape, jnp.float32)
    grad_values = jnp.zeros(value_rows.shape, jnp.float32)
    for begin_row in range(0, SEQ_LEN, block_size):
        stop_key = key_stop(begin_row, block_size)
        scores = block_scores(queries, key_rows, lengths, begin_row, block_size, stop_key)
        probability = jnp.exp(scores - log_sums[:, :, begin_row : begin_row + block_size, None])
        grad_block = grad_attn[:, begin_row : begin_row + block_size]
        grad_prob = jnp.einsum(
            "sqhe,skhe->shqk",
            grad_block,
            value_rows[:, :stop_key],
            preferred_element_type=jnp.float32,
        )
        row_delta = jnp.sum(probability * grad_prob, axis=-1, keepdims=True)
        grad_scores = (probability * (grad_prob - row_delta)).astype(jnp.bfloat16)
        grad_queries.append(
            jnp.einsum(
                "shqk,skhe->sqhe",
                grad_scores,
                key_rows[:, :stop_key],
                preferred_element_type=jnp.float32,
            )
            * scaling
        )
        key_part = (
            jnp.einsum(
                "shqk,sqhe->skhe",
                grad_scores,
                queries[:, begin_row : begin_row + block_size],
                preferred_element_type=jnp.float32,
            )
            * scaling
        )
        grad_keys = grad_keys.at[:, :stop_key].add(key_part)
        value_part = jnp.einsum(
            "shqk,sqhe->skhe",
            probability.astype(jnp.bfloat16),
            grad_block,
            preferred_element_type=jnp.float32,
        )
        grad_values = grad_values.at[:, :stop_key].add(value_part)
    return (jnp.concatenate(grad_queries, axis=1), grad_keys, grad_values)


def placed(segment, total_width, part_index):
    empty = jnp.zeros((total_width,), jnp.float32)
    return lax.dynamic_update_slice_in_dim(empty, segment, part_index * segment.shape[0], 0)


def body(
    inputs,
    prefix,
    cotangent,
    w_query,
    w_key,
    w_value,
    w_out,
    w_up,
    w_down,
    b_query,
    b_value,
    b_out,
    b_up,
    b_down,
    gain_one,
    shift_one,
    gain_two,
    shift_two,
):
    float_type = jnp.float32
    half_type = jnp.bfloat16
    part_index = lax.axis_index("tensor")
    full_query, full_key, full_value, full_out = (
        lax.all_gather(w_query, "dp", axis=0, tiled=True),
        lax.all_gather(w_key, "dp", axis=0, tiled=True),
        lax.all_gather(w_value, "dp", axis=0, tiled=True),
        lax.all_gather(w_out, "dp", axis=1, tiled=True),
    )
    full_up, full_down = (
        lax.all_gather(w_up, "dp", axis=0, tiled=True),
        lax.all_gather(w_down, "dp", axis=1, tiled=True),
    )
    head_width = full_query.shape[1]
    ff_width = full_up.shape[1]
    heads_here = head_width // HEAD
    bias_query = lax.dynamic_slice_in_dim(
        b_query.astype(float_type), part_index * head_width, head_width
    )
    bias_value = lax.dynamic_slice_in_dim(
        b_value.astype(float_type), part_index * head_width, head_width
    )
    bias_up = lax.dynamic_slice_in_dim(b_up.astype(float_type), part_index * ff_width, ff_width)
    gain_first = gain_one.astype(float_type)
    shift_first = shift_one.astype(float_type)
    gain_second = gain_two.astype(float_type)
    shift_second = shift_two.astype(float_type)
    in_rows = inputs.astype(float_type)
    norm_first = layer_norm(in_rows, gain_first, shift_first)
    normed_one = lax.all_gather(norm_first.astype(half_type), "tensor", axis=0, tiled=True)
    seq_count = normed_one.shape[0] // SEQ_LEN
    stacked = jnp.concatenate([full_query, full_key, full_value], axis=1)
    projected = dot_right(normed_one, stacked)
    shape_four = (seq_count, SEQ_LEN, heads_here, HEAD)
    queries = (projected[:, :head_width] + bias_query).astype(half_type).reshape(shape_four)
    key_rows = projected[:, head_width : 2 * head_width].astype(half_type).reshape(shape_four)
    value_rows = (projected[:, 2 * head_width :] + bias_value).astype(half_type).reshape(shape_four)
    attended, log_sums = attend_forward(queries, key_rows, value_rows, prefix)
    attended = attended.reshape(-1, head_width).astype(half_type)
    attn_piece = lax.psum_scatter(
        dot_right(attended, full_out), "tensor", scatter_dimension=0, tiled=True
    )
    middle = in_rows + attn_piece + b_out.astype(float_type)
    norm_second = layer_norm(middle, gain_second, shift_second)
    normed_two = lax.all_gather(norm_second.astype(half_type), "tensor", axis=0, tiled=True)
    pre_act = dot_right(normed_two, full_up) + bias_up
    activated = gelu_exact(pre_act).astype(half_type)
    ff_piece = lax.psum_scatter(
        dot_right(activated, full_down).astype(jnp.bfloat16),
        "tensor",
        scatter_dimension=0,
        tiled=True,
    ).astype(jnp.float32)
    result = (middle + ff_piece + b_down.astype(float_type)).astype(half_type)
    grad_result = cotangent.astype(float_type)
    grad_ff_rows = lax.all_gather(cotangent, "tensor", axis=0, tiled=True)
    grad_act = dot_back(grad_ff_rows, full_down)
    grad_down = dot_over_rows(activated, grad_ff_rows)
    grad_pre = jax.vjp(gelu_exact, pre_act)[1](grad_act)[0].astype(half_type)
    grad_bias_up = jnp.sum(grad_pre, axis=0, dtype=float_type)
    grad_up = dot_over_rows(normed_two, grad_pre)
    grad_norm_two = lax.psum_scatter(
        dot_back(grad_pre, full_up), "tensor", scatter_dimension=0, tiled=True
    )
    norm_two_back = jax.vjp(layer_norm, middle, gain_second, shift_second)[1](grad_norm_two)
    grad_middle = grad_result + norm_two_back[0]
    grad_attn_rows = lax.all_gather(grad_middle.astype(half_type), "tensor", axis=0, tiled=True)
    grad_attended = dot_back(grad_attn_rows, full_out).astype(half_type)
    grad_out_proj = dot_over_rows(attended, grad_attn_rows)
    grad_queries, grad_keys, grad_values = attend_backward(
        queries, key_rows, value_rows, grad_attended.reshape(shape_four), log_sums, prefix
    )
    grads_joined = jnp.concatenate(
        [
            grad_queries.reshape(-1, head_width),
            grad_keys.reshape(-1, head_width),
            grad_values.reshape(-1, head_width),
        ],
        axis=1,
    ).astype(half_type)
    grad_stacked = dot_over_rows(normed_one, grads_joined)
    column_sums = jnp.sum(grads_joined, axis=0, dtype=float_type)
    grad_norm_one = lax.psum_scatter(
        dot_back(grads_joined, stacked).astype(jnp.bfloat16),
        "tensor",
        scatter_dimension=0,
        tiled=True,
    ).astype(jnp.float32)
    norm_one_back = jax.vjp(layer_norm, in_rows, gain_first, shift_first)[1](grad_norm_one)
    grad_input = grad_middle + norm_one_back[0]
    grad_query = grad_stacked[:, :head_width]
    grad_key = grad_stacked[:, head_width : 2 * head_width]
    grad_value = grad_stacked[:, 2 * head_width :]
    shard_query, shard_key, shard_value, shard_out, shard_up, shard_down = (
        lax.psum_scatter(grad_query, "dp", scatter_dimension=0, tiled=True),
        lax.psum_scatter(grad_key, "dp", scatter_dimension=0, tiled=True),
        lax.psum_scatter(grad_value, "dp", scatter_dimension=0, tiled=True),
        lax.psum_scatter(grad_out_proj, "dp", scatter_dimension=1, tiled=True),
        lax.psum_scatter(grad_up, "dp", scatter_dimension=0, tiled=True),
        lax.psum_scatter(grad_down, "dp", scatter_dimension=1, tiled=True),
    )
    vector_sums = lax.psum(
        (
            placed(column_sums[:head_width], b_query.shape[0], part_index),
            placed(column_sums[2 * head_width :], b_value.shape[0], part_index),
            jnp.sum(grad_middle, axis=0),
            placed(grad_bias_up, b_up.shape[0], part_index),
            jnp.sum(grad_result, axis=0),
            norm_one_back[1],
            norm_one_back[2],
            norm_two_back[1],
            norm_two_back[2],
        ),
        ("dp", "tensor"),
    )
    return (
        result,
        grad_input,
        shard_query,
        shard_key,
        shard_value,
        shard_out,
        shard_up,
        shard_down,
        vector_sums[0],
        vector_sums[1],
        vector_sums[2],
        vector_sums[3],
        vector_sums[4],
        vector_sums[5],
        vector_sums[6],
        vector_sums[7],
        vector_sums[8],
    )


def solution(mesh):
    placed = (
        P(("dp", "tensor"), None),
        P("dp"),
        P(("dp", "tensor"), None),
        P("dp", "tensor"),
        P("dp", "tensor"),
        P("dp", "tensor"),
        P("tensor", "dp"),
        P("dp", "tensor"),
        P("tensor", "dp"),
        P(),
        P(),
        P(),
        P(),
        P(),
        P(),
        P(),
        P(),
        P(),
    )
    return jax.shard_map(
        body,
        mesh=mesh,
        in_specs=placed,
        out_specs=(
            P(("dp", "tensor"), None),
            P(("dp", "tensor"), None),
            P("dp", "tensor"),
            P("dp", "tensor"),
            P("dp", "tensor"),
            P("tensor", "dp"),
            P("dp", "tensor"),
            P("tensor", "dp"),
            P(),
            P(),
            P(),
            P(),
            P(),
            P(),
            P(),
            P(),
            P(),
        ),
        check_vma=False,
    )
```

profile of v0, /device:TPU:0, one launch (start us, length us, event | category | flops | bytes accessed | tf_op | source)
XLA Modules:
  0.0 988.7 jit_solution(17090238682944329113)
XLA Ops:
  15.7 11.1 %all_gather.34 = bf16[192,768]{0,1:T(8,128)(2,1)S(1)} all-gather(bf16[192,96]{0,1:T(8,128)(2,1)S(1)} %copy.81), channel_id=1, replica_groups=mesh['dp'=8,'tensor'=4] {'dp'}, dimensions={1}, use_global_device_ids=true | all-gather | bytes 331776 | tf_op jit(solution)/shard_map/all_gather | solution.py:171
  26.8 9.5 all_gather.31
  36.3 8.6 all_gather.32
  44.9 9.5 all_gather.33
  57.6 24.0 %all-gather.7.cloned.1.call-done = bf16[2048,768]{1,0:T(8,128)(2,1)} async-done(((bf16[512,768]{1,0:T(8,128)(2,1)}), bf16[2048,768]{1,0:T(8,128)(2,1)}) %all-gather.7.cloned.1.call-update) | async-done | bytes 3145744 | tf_op jit(solution)/shard_map/all_gather | solution.py:193
  81.7 4.1 fusion.65
  94.9 4.2 fusion.83
  118.7 108.3 %reduce-scatter.19.cloned.1.call-done = f32[512,768]{1,0:T(8,128)} async-done(((f32[2048,768]{1,0:T(8,128)}), f32[512,768]{1,0:T(8,128)}) %reduce-scatter.19.cloned.1.call-update) | async-done | bytes 1572880 | tf_op jit(solution)/shard_map/reduce_scatter | solution.py:203
  233.4 60.8 %all-gather.9.cloned.1.call-done = bf16[2048,768]{1,0:T(8,128)(2,1)} async-done(((bf16[512,768]{1,0:T(8,128)(2,1)}), bf16[2048,768]{1,0:T(8,128)(2,1)}) %all-gather.9.cloned.1.call-update) | async-done | bytes 3145744 | tf_op jit(solution)/shard_map/all_gather | solution.py:208
  294.2 7.5 fusion.86
  301.7 16.7 %all-gather.13.cloned.1.call-done = bf16[768,768]{0,1:T(8,128)(2,1)} async-done(((bf16[768,96]{0,1:T(8,128)(2,1)}), bf16[768,768]{0,1:T(8,128)(2,1)}) %all-gather.13.cloned.1.call-update) | async-done | bytes 1179664 | tf_op jit(solution)/shard_map/all_gather | solution.py:175
  318.4 64.9 %all-gather.15.cloned.1.call-done = bf16[2048,768]{1,0:T(8,128)(2,1)} async-done(((bf16[512,768]{1,0:T(8,128)(2,1)}), bf16[2048,768]{1,0:T(8,128)(2,1)}) %all-gather.15.cloned.1.call-update) | async-done | bytes 3145744 | tf_op jit(solution)/shard_map/all_gather | solution.py:219
  383.3 20.6 %convert_reduce_fusion = (f32[768]{0:T(1024)}, bf16[2048,768]{1,0:T(8,128)(2,1)S(1)}, f32[2048,768]{1,0:T(8,128)}) fusion(f32[2048,768]{1,0:T(8,128)} %fusion.86, f32[768]{0:T(1024)} %dynamic-slice_convert_fusion, bf16[2048,768]{1,0:T(8,128)(2,1)} %all-gather.15.cloned.1.call-done, bf16[768,768]{0,1:T(8,128)(2,1)} %all-gather.13.cloned.1.call-done), kind=kOutput, calls=%fused_computation.11 | convolution fusion | flops 2533883136 | bytes 20060160 | tf_op jit(solution)/shard_map/dot_general | solution.py:29
  405.6 4.6 fusion.87
  410.3 5.7 multiply_convert_fusion.2
  423.0 96.7 %reduce-scatter.23.cloned.1.call-done = f32[512,768]{1,0:T(8,128)} async-done(((f32[2048,768]{1,0:T(8,128)}), f32[512,768]{1,0:T(8,128)}) %reduce-scatter.23.cloned.1.call-update) | async-done | bytes 1572880 | tf_op jit(solution)/shard_map/reduce_scatter | solution.py:225
  522.9 60.1 %reduce-scatter.21.cloned.1.call-done = bf16[512,768]{1,0:T(8,128)(2,1)} async-done(((bf16[2048,768]{1,0:T(8,128)(2,1)}), bf16[512,768]{1,0:T(8,128)(2,1)}) %reduce-scatter.21.cloned.1.call-update) | async-done | bytes 786448 | tf_op jit(solution)/shard_map/reduce_scatter | solution.py:211
  588.9 63.1 %all-gather.17.cloned.1.call-done = bf16[2048,768]{1,0:T(8,128)(2,1)} async-done(((bf16[512,768]{1,0:T(8,128)(2,1)}), bf16[2048,768]{1,0:T(8,128)(2,1)}) %all-gather.17.cloned.1.call-update) | async-done | bytes 3145744 | tf_op jit(solution)/shard_map/all_gather | solution.py:230
  659.2 4.0 fusion.38
  663.2 4.4 multiply_reduce_fusion.1
  676.5 10.6 %multiply_reduce_fusion = (f32[2,3,512]{2,1,0:T(4,128)S(1)}, f32[2,3,512,1024]{3,2,1,0:T(8,128)}) fusion(f32[2,3,512,1024]{3,2,1,0:T(8,128)} %copy-done, f32[2,3,512]{2,1,0:T(4,128)S(1)} %log_add_fusion, bf16[2,1024,3,64]{1,0,3,2:T(2,128)(2,1)S(1)} %reshape.334, bf16[2,512,3,64]{1,0,3,2:T(2,128)(2,1)S(1)} %get-tuple-element.165), kind=kOutput, calls=%fused_computation.1 | convolution fusion | flops 412087296 | bytes 26370048 | tf_op jit(solution)/shard_map/sqhe,skhe->shqk/dot_general | solution.py:102
  687.1 6.0 fusion.34
  694.2 6.4 multiply_convert_fusion
  707.1 4.5 convolution_convert_fusion
  711.9 6.9 fusion.89
  718.9 6.9 fusion.88
  738.1 34.4 %reduce-scatter.25.cloned.1.call-done = bf16[512,768]{1,0:T(8,128)(2,1)} async-done(((bf16[2048,768]{1,0:T(8,128)(2,1)}), bf16[512,768]{1,0:T(8,128)(2,1)}) %reduce-scatter.25.cloned.1.call-update) | async-done | bytes 786448 | tf_op jit(solution)/shard_map/reduce_scatter | solution.py:246
  778.4 41.5 %all-reduce.2 = (f32[768]{0:T(1024)}, f32[768]{0:T(1024)}, f32[768]{0:T(1024)}, f32[3072]{0:T(1024)}, f32[768]{0:T(1024)}, /*index=5*/f32[768]{0:T(1024)}, f32[768]{0:T(1024)}, f32[768]{0:T(1024)}, f32[768]{0:T(1024)}) all-reduce(f32[768]{0:T(1024)S(1)} %slice_dynamic-update-slice_fusion.1, ...), channel_id=1, replica_groups=mesh['dp'=8,'tensor'=4] {'dp','tensor'}, use_global_device_ids=true, to_apply=%region_25.26 | all-reduce | flops 9216 | bytes 73728 | tf_op jit(solution)/shard_map/psum | solution.py:265
  819.9 45.2 %reduce-scatter.27.cloned.1.call-done = f32[96,768]{1,0:T(8,128)} async-done(((f32[768,768]{1,0:T(8,128)}), f32[96,768]{1,0:T(8,128)}) %reduce-scatter.27.cloned.1.call-update) | async-done | bytes 294928 | tf_op jit(solution)/shard_map/reduce_scatter | solution.py:262
  865.2 38.5 %reduce-scatter.35.cloned.1.call-done = f32[96,192]{1,0:T(8,128)} async-done(((f32[768,192]{1,0:T(8,128)}), f32[96,192]{1,0:T(8,128)}) %reduce-scatter.35.cloned.1.call-update) | async-done | bytes 73744
  903.7 38.7 %reduce-scatter.33.cloned.1.call-done = f32[96,192]{1,0:T(8,128)} async-done(((f32[768,192]{1,0:T(8,128)}), f32[96,192]{1,0:T(8,128)}) %reduce-scatter.33.cloned.1.call-update) | async-done | bytes 73744
  942.4 38.5 %reduce-scatter.31.cloned.1.call-done = f32[96,192]{1,0:T(8,128)} async-done(((f32[768,192]{1,0:T(8,128)}), f32[96,192]{1,0:T(8,128)}) %reduce-scatter.31.cloned.1.call-update) | async-done | bytes 73744
  (270 shorter events, 104.9 us)
Async XLA Ops:
  8.1 28.2 %copy-start.46 = (bf16[96,192]{1,0:T(8,128)(2,1)S(1)}, bf16[96,192]{1,0:T(8,128)(2,1)}, u32[]{:S(2)}) copy-start(bf16[96,192]{1,0:T(8,128)(2,1)} %param.34) | copy-start | bytes 110596
  8.1 36.8 %copy-start.47 = (bf16[96,192]{1,0:T(8,128)(2,1)S(1)}, bf16[96,192]{1,0:T(8,128)(2,1)}, u32[]{:S(2)}) copy-start(bf16[96,192]{1,0:T(8,128)(2,1)} %param.35) | copy-start | bytes 110596
  8.1 46.8 %copy-start.62 = (s32[2]{0:T(128)S(1)}, s32[2]{0:T(128)}, u32[]{:S(2)}) copy-start(s32[2]{0:T(128)} %param.31) | copy-start | bytes 28
  8.1 73.6 %all-gather.7.cloned.1.call-start = ((), (), s32[]{:S(2)}) async-start(), calls=%async_computation.10 | async-start | bytes 3932160 | tf_op jit(solution)/shard_map/all_gather | solution.py:193
  15.3 211.6 %reduce-scatter.19.cloned.1.call-start = ((), (), s32[]{:S(2)}) async-start(), calls=%async_computation.11 | async-start | bytes 7864320 | tf_op jit(solution)/shard_map/reduce_scatter | solution.py:203
  36.3 45.4 %copy-start.26 = (bf16[768,192]{1,0:T(8,128)(2,1)}, bf16[768,192]{1,0:T(8,128)(2,1)S(1)}, u32[]{:S(2)}) copy-start(bf16[768,192]{1,0:T(8,128)(2,1)S(1)} %all_gather.31) | copy-start | bytes 884740
  44.9 36.8 %copy-start.28 = (bf16[768,192]{1,0:T(8,128)(2,1)}, bf16[768,192]{1,0:T(8,128)(2,1)S(1)}, u32[]{:S(2)}) copy-start(bf16[768,192]{1,0:T(8,128)(2,1)S(1)} %all_gather.32) | copy-start | bytes 884740
  54.4 31.3 %copy-start.30 = (bf16[768,192]{1,0:T(8,128)(2,1)}, bf16[768,192]{1,0:T(8,128)(2,1)S(1)}, u32[]{:S(2)}) copy-start(bf16[768,192]{1,0:T(8,128)(2,1)S(1)} %all_gather.33) | copy-start | bytes 884740
  117.4 109.6 %copy-start.2 = (bf16[512,768]{1,0:T(8,128)(2,1)S(1)}, bf16[512,768]{1,0:T(8,128)(2,1)}, u32[]{:S(2)}) copy-start(bf16[512,768]{1,0:T(8,128)(2,1)} %param.30) | copy-start | bytes 2359300
  117.4 116.0 %all-gather.11.cloned.1.call-start = ((), (), s32[]{:S(2)}) async-start(), calls=%async_computation.13 | async-start | bytes 1327104 | tf_op jit(solution)/shard_map/all_gather | solution.py:174
  118.0 176.2 %all-gather.9.cloned.1.call-start = ((), (), s32[]{:S(2)}) async-start(), calls=%async_computation.12 | async-start | bytes 3932160 | tf_op jit(solution)/shard_map/all_gather | solution.py:208
  230.2 88.1 %all-gather.13.cloned.1.call-start = ((), (), s32[]{:S(2)}) async-start(), calls=%async_computation.14 | async-start | bytes 1327104 | tf_op jit(solution)/shard_map/all_gather | solution.py:175
  230.8 152.5 %all-gather.15.cloned.1.call-start = ((), (), s32[]{:S(2)}) async-start(), calls=%async_computation.16 | async-start | bytes 3932160 | tf_op jit(solution)/shard_map/all_gather | solution.py:219
  231.6 288.1 %reduce-scatter.23.cloned.1.call-start = ((), (), s32[]{:S(2)}) async-start(), calls=%async_computation.17 | async-start | bytes 7864320 | tf_op jit(solution)/shard_map/reduce_scatter | solution.py:225
  410.2 172.7 %reduce-scatter.21.cloned.1.call-start = ((), (), s32[]{:S(2)}) async-start(), calls=%async_computation.15 | async-start | bytes 3932160 | tf_op jit(solution)/shard_map/reduce_scatter | solution.py:211
  421.6 230.4 %all-gather.17.cloned.1.call-start = ((), (), s32[]{:S(2)}) async-start(), calls=%async_computation.18 | async-start | bytes 3932160 | tf_op jit(solution)/shard_map/all_gather | solution.py:230
  586.3 69.7 %copy-start.53 = (f32[512]{0:T(512)}, f32[512]{0:T(512)S(1)}, u32[]{:S(2)}) copy-start(f32[512]{0:T(512)S(1)} %negate_multiply_fusion.2) | copy-start | bytes 6148
  588.6 147.8 %reduce-scatter.37.cloned.1.call-start = ((), (), s32[]{:S(2)}) async-start(), calls=%async_computation.25 | async-start | bytes 884736
  588.9 74.3 %copy-start.32 = (f32[2,3,512]{2,1,0:T(4,128)}, f32[2,3,512]{2,1,0:T(4,128)S(1)}, u32[]{:S(2)}) copy-start(f32[2,3,512]{2,1,0:T(4,128)S(1)} %log_add_fusion.1) | copy-start | bytes 36868
  676.2 96.3 %reduce-scatter.25.cloned.1.call-start = ((), (), s32[]{:S(2)}) async-start(), calls=%async_computation.19 | async-start | bytes 3932160 | tf_op jit(solution)/shard_map/reduce_scatter | solution.py:246
  711.6 108.3 %reduce-scatter.29.cloned.1.call-start = ((), (), s32[]{:S(2)}) async-start(), calls=%async_computation.21 | async-start | bytes 2654208 | tf_op jit(solution)/shard_map/reduce_scatter | solution.py:263
  718.9 146.3 %reduce-scatter.27.cloned.1.call-start = ((), (), s32[]{:S(2)}) async-start(), calls=%async_computation.20 | async-start | bytes 2654208 | tf_op jit(solution)/shard_map/reduce_scatter | solution.py:262
  725.8 177.8 %reduce-scatter.35.cloned.1.call-start = ((), (), s32[]{:S(2)}) async-start(), calls=%async_computation.24 | async-start | bytes 884736
  731.1 211.2 %reduce-scatter.33.cloned.1.call-start = ((), (), s32[]{:S(2)}) async-start(), calls=%async_computation.23 | async-start | bytes 884736
  731.2 41.3 %copy-start.34 = (f32[768]{0:T(1024)S(1)}, f32[768]{0:T(1024)}, u32[]{:S(2)}) copy-start(f32[768]{0:T(1024)} %copy-done.33) | copy-start | bytes 9220
  731.2 41.3 %copy-start.36 = (f32[512]{0:T(512)S(1)}, f32[512]{0:T(512)}, u32[]{:S(2)}) copy-start(f32[512]{0:T(512)} %copy-done.35) | copy-start | bytes 6148
  732.4 248.5 %reduce-scatter.31.cloned.1.call-start = ((), (), s32[]{:S(2)}) async-start(), calls=%async_computation.22 | async-start | bytes 884736
  732.7 41.5 %copy-start.52 = (f32[512]{0:T(512)S(1)}, f32[512]{0:T(512)}, u32[]{:S(2)}) copy-start(f32[512]{0:T(512)} %copy-done.51) | copy-start | bytes 6148
  732.7 41.5 %copy-start.50 = (f32[512]{0:T(512)S(1)}, f32[512]{0:T(512)}, u32[]{:S(2)}) copy-start(f32[512]{0:T(512)} %copy-done.49) | copy-start | bytes 6148
  733.9 42.5 %copy-start.4 = (f32[512,768]{1,0:T(8,128)S(1)}, f32[512,768]{1,0:T(8,128)}, u32[]{:S(2)}) copy-start(f32[512,768]{1,0:T(8,128)} %copy-done.3) | copy-start | bytes 4718596
  733.9 42.5 %copy-start.9 = (bf16[512,768]{1,0:T(8,128)(2,1)S(1)}, bf16[512,768]{1,0:T(8,128)(2,1)}, u32[]{:S(2)}) copy-start(bf16[512,768]{1,0:T(8,128)(2,1)} %param.32) | copy-start | bytes 2359300
  733.9 42.5 %copy-start.54 = (f32[512]{0:T(512)S(1)}, f32[512]{0:T(512)}, u32[]{:S(2)}) copy-start(f32[512]{0:T(512)} %copy-done.53) | copy-start | bytes 6148
  (57 other events, 274.2 us)
Sparse Core Ops, SparseCore 0:
  15.5 66.1 all-gather.6
  117.5 109.4 reduce-scatter.18
  588.7 63.2 all-gather.16
Sparse Core Ops, SparseCore 1:
  119.8 22.4 all-gather.10
  230.3 63.8 all-gather.8
  295.9 22.4 all-gather.12
  320.0 63.3 all-gather.14
  410.3 109.3 reduce-scatter.22
  522.0 60.9 reduce-scatter.20
  676.3 33.5 reduce-scatter.36
  712.0 60.4 reduce-scatter.24
  776.3 42.3 reduce-scatter.28
  822.6 42.5 reduce-scatter.26
  868.8 34.9 reduce-scatter.34
  907.4 34.9 reduce-scatter.32
  945.9 34.9 reduce-scatter.30
where the time goes:
time: 997 us; the launch traced here: 989 us
  waiting for transfers between devices  692 us (69%)
  matrix products  114 us (11%)
  blocking collectives  80.2 us (8%)
  other arithmetic  53 us (5%)
  local copies, waits for them, and re-layouts  30.8 us (3%)
  between operations  17.1 us (2%)
    unnamed x20, waiting for transfers between devices  118 us
    reduce_scatter x1, waiting for transfers between devices, body(): lax.psum_scatter(dot_right(attended, full_out), 'tensor', scatter_dimensi...  108 us
    reduce_scatter x1, waiting for transfers between devices, body(): lax.psum_scatter(dot_back(grad_pre, full_up), 'tensor', scatter_dimension...  96.7 us
    all_gather x1, waiting for transfers between devices, body(): grad_ff_rows = lax.all_gather(cotangent, 'tensor', axis=0, tiled=True)  64.9 us
    all_gather x1, waiting for transfers between devices, body(): lax.all_gather(grad_middle.astype(half_type), 'tensor', axis=0, tiled=True)  63.1 us
    all_gather x1, waiting for transfers between devices, body(): lax.all_gather(norm_second.astype(half_type), 'tensor', axis=0, tiled=True)  60.8 us
    reduce_scatter x1, waiting for transfers between devices, body(): lax.psum_scatter(dot_right(activated, full_down).astype(jnp.bfloat16), 't...  60.1 us
    reduce_scatter x1, waiting for transfers between devices, body(): lax.psum_scatter(grad_up, 'dp', scatter_dimension=0, tiled=True)  45.2 us
  transfers between devices with their start and end apart: 16, of which 13 were waited for; matrix products, arithmetic and copies ran while one was open for 10% of the time, Pallas kernels for 0%

commit v1 on v0

v1 whole, which is shorter than its diff:
```python
import jax
import jax.numpy as jnp
from jax import lax
from jax.sharding import PartitionSpec as P

HEAD = 64
SEQ_LEN = 1024

norm_eps = 1e-12
masked_score = -1e30


def layer_norm(values, norm_gain, norm_shift):
    center = values - jnp.mean(values, axis=-1, keepdims=True)
    spread = jnp.mean(center * center, axis=-1, keepdims=True)
    return center * lax.rsqrt(spread + norm_eps) * norm_gain + norm_shift


def gelu_exact(values):
    return jax.nn.gelu(values, approximate=False)


def dot_right(first_op, second_op):
    return jnp.dot(first_op, second_op, preferred_element_type=jnp.float32)


def dot_back(first_op, second_op):
    return lax.dot_general(
        first_op, second_op, (((1,), (1,)), ((), ())), preferred_element_type=jnp.float32
    )


def dot_over_rows(first_op, second_op):
    return lax.dot_general(
        first_op, second_op, (((0,), (0,)), ((), ())), preferred_element_type=jnp.float32
    )


AXES = ("dp", "tensor")


def gather_rows_cols(shard, dp, tp):
    r, c = shard.shape
    full = lax.all_gather(shard, AXES, axis=0, tiled=False)
    return full.reshape(dp, tp, r, c).transpose(0, 2, 1, 3).reshape(dp * r, tp * c)


def gather_cols_rows(shard, dp, tp):
    r, c = shard.shape
    full = lax.all_gather(shard, AXES, axis=0, tiled=False)
    return full.reshape(dp, tp, r, c).transpose(1, 2, 0, 3).reshape(tp * r, dp * c)


def blocks_rows_cols(grad, dp, tp):
    rows, cols = grad.shape
    r, c = rows // dp, cols // tp
    return grad.reshape(dp, r, tp, c).transpose(0, 2, 1, 3).reshape(dp * tp, r, c)


def blocks_cols_rows(grad, dp, tp):
    rows, cols = grad.shape
    r, c = rows // tp, cols // dp
    return grad.reshape(tp, r, dp, c).transpose(2, 0, 1, 3).reshape(dp * tp, r, c)


def scatter_blocks(blocks):
    return lax.psum_scatter(blocks, AXES, scatter_dimension=0, tiled=False)


def summed_everywhere(vectors):
    joined = jnp.concatenate(vectors)
    total = jnp.sum(lax.all_gather(joined, AXES, axis=0, tiled=False), axis=0)
    out = []
    start = 0
    for v in vectors:
        out.append(total[start : start + v.shape[0]])
        start += v.shape[0]
    return out


def scores_of(queries, key_rows, qpos, kpos, prefix_len):
    scaling = HEAD ** (-0.5)
    scores = jnp.einsum("qhe,khe->hqk", queries, key_rows, preferred_element_type=jnp.float32) * scaling
    visible = (kpos[None, :] <= qpos[:, None]) | (kpos[None, :] < prefix_len)
    return jnp.where(visible[None], scores, masked_score)


def body(
    inputs,
    prefix,
    cotangent,
    w_query,
    w_key,
    w_value,
    w_out,
    w_up,
    w_down,
    b_query,
    b_value,
    b_out,
    b_up,
    b_down,
    gain_one,
    shift_one,
    gain_two,
    shift_two,
):
    f32 = jnp.float32
    bf16 = jnp.bfloat16
    dp = lax.axis_size("dp")
    tp = lax.axis_size("tensor")
    t_index = lax.axis_index("tensor")
    rows = inputs.shape[0]
    pieces = SEQ_LEN // rows
    assert pieces == 2
    half = t_index % pieces
    seq_here = (t_index * rows) // SEQ_LEN
    prefix_len = lax.dynamic_index_in_dim(prefix, seq_here, keepdims=False)
    pos_own = half * rows + lax.iota(jnp.int32, rows)
    pos_oth = (1 - half) * rows + lax.iota(jnp.int32, rows)
    to_second = [(t, t + 1) for t in range(0, tp, 2)]
    to_first = [(t + 1, t) for t in range(0, tp, 2)]

    full_query = gather_rows_cols(w_query, dp, tp)
    full_key = gather_rows_cols(w_key, dp, tp)
    full_value = gather_rows_cols(w_value, dp, tp)
    full_out = gather_cols_rows(w_out, dp, tp)
    full_up = gather_rows_cols(w_up, dp, tp)
    full_down = gather_cols_rows(w_down, dp, tp)
    width = full_query.shape[1]
    heads = width // HEAD

    gain_first = gain_one.astype(f32)
    shift_first = shift_one.astype(f32)
    gain_second = gain_two.astype(f32)
    shift_second = shift_two.astype(f32)

    in_rows = inputs.astype(f32)
    normed_one = layer_norm(in_rows, gain_first, shift_first).astype(bf16)
    key_rows = dot_right(normed_one, full_key).astype(bf16)
    value_rows = (dot_right(normed_one, full_value) + b_value.astype(f32)).astype(bf16)
    queries = (dot_right(normed_one, full_query) + b_query.astype(f32)).astype(bf16)
    shape3 = (rows, heads, HEAD)
    q3 = queries.reshape(shape3)
    k3 = key_rows.reshape(shape3)
    v3 = value_rows.reshape(shape3)
    k_oth, v_oth = lax.ppermute((k3, v3), "tensor", to_second)

    s_own = scores_of(q3, k3, pos_own, pos_own, prefix_len)
    s_oth = scores_of(q3, k_oth, pos_own, pos_oth, prefix_len)
    row_top = jnp.maximum(jnp.max(s_own, axis=-1, keepdims=True), jnp.max(s_oth, axis=-1, keepdims=True))
    e_own = jnp.exp(s_own - row_top)
    e_oth = jnp.exp(s_oth - row_top)
    row_total = jnp.sum(e_own, axis=-1, keepdims=True) + jnp.sum(e_oth, axis=-1, keepdims=True)
    p_own = (e_own / row_total).astype(bf16)
    p_oth = (e_oth / row_total).astype(bf16)
    attended = jnp.einsum("hqk,khe->qhe", p_own, v3, preferred_element_type=f32) + jnp.einsum(
        "hqk,khe->qhe", p_oth, v_oth, preferred_element_type=f32
    )
    log_sums = row_top + jnp.log(row_total)
    attended = attended.reshape(rows, width).astype(bf16)
    q_rcv, lse_rcv = lax.ppermute((q3, log_sums), "tensor", to_first)

    middle = in_rows + dot_right(attended, full_out) + b_out.astype(f32)
    normed_two = layer_norm(middle, gain_second, shift_second).astype(bf16)
    pre_act = dot_right(normed_two, full_up) + b_up.astype(f32)
    activated = gelu_exact(pre_act).astype(bf16)
    result = (middle + dot_right(activated, full_down) + b_down.astype(f32)).astype(bf16)

    grad_result = cotangent.astype(f32)
    down_blocks = blocks_cols_rows(dot_over_rows(activated, cotangent), dp, tp)
    grad_act = dot_back(cotangent, full_down)
    down_blocks, grad_act = lax.optimization_barrier((down_blocks, grad_act))
    shard_down = scatter_blocks(down_blocks)
    grad_pre = jax.vjp(gelu_exact, pre_act)[1](grad_act)[0].astype(bf16)
    up_blocks = blocks_rows_cols(dot_over_rows(normed_two, grad_pre), dp, tp)
    grad_norm_two = dot_back(grad_pre, full_up)
    up_blocks, grad_norm_two = lax.optimization_barrier((up_blocks, grad_norm_two))
    shard_up = scatter_blocks(up_blocks)
    norm_two_back = jax.vjp(layer_norm, middle, gain_second, shift_second)[1](grad_norm_two)
    grad_middle = grad_result + norm_two_back[0]
    early_sums = summed_everywhere(
        [
            jnp.sum(grad_middle, axis=0),
            jnp.sum(grad_pre, axis=0, dtype=f32),
            jnp.sum(grad_result, axis=0),
            norm_two_back[1],
            norm_two_back[2],
        ]
    )
    grad_attn_rows = grad_middle.astype(bf16)
    out_blocks = blocks_cols_rows(dot_over_rows(attended, grad_attn_rows), dp, tp)
    grad_attended = dot_back(grad_attn_rows, full_out).astype(bf16)
    out_blocks, grad_attended = lax.optimization_barrier((out_blocks, grad_attended))
    shard_out = scatter_blocks(out_blocks)
    do3 = grad_attended.reshape(shape3)

    scaling = HEAD ** (-0.5)
    prob_own = jnp.exp(s_own - log_sums)
    prob_oth = jnp.exp(s_oth - log_sums)
    dp_own = jnp.einsum("qhe,khe->hqk", do3, v3, preferred_element_type=f32)
    dp_oth = jnp.einsum("qhe,khe->hqk", do3, v_oth, preferred_element_type=f32)
    delta = jnp.sum(prob_own * dp_own, axis=-1, keepdims=True) + jnp.sum(
        prob_oth * dp_oth, axis=-1, keepdims=True
    )
    do_rcv, delta_rcv = lax.ppermute((do3, delta), "tensor", to_first)
    ds_own = (prob_own * (dp_own - delta)).astype(bf16)
    ds_oth = (prob_oth * (dp_oth - delta)).astype(bf16)
    dq = (
        jnp.einsum("hqk,khe->qhe", ds_own, k3, preferred_element_type=f32)
        + jnp.einsum("hqk,khe->qhe", ds_oth, k_oth, preferred_element_type=f32)
    ) * scaling
    dk = jnp.einsum("hqk,qhe->khe", ds_own, q3, preferred_element_type=f32)
    dv = jnp.einsum("hqk,qhe->khe", prob_own.astype(bf16), do3, preferred_element_type=f32)
    s_x = scores_of(q_rcv, k3, pos_oth, pos_own, prefix_len)
    prob_x = jnp.exp(s_x - lse_rcv)
    dp_x = jnp.einsum("qhe,khe->hqk", do_rcv, v3, preferred_element_type=f32)
    ds_x = (prob_x * (dp_x - delta_rcv)).astype(bf16)
    dk = (dk + jnp.einsum("hqk,qhe->khe", ds_x, q_rcv, preferred_element_type=f32)) * scaling
    dv = dv + jnp.einsum("hqk,qhe->khe", prob_x.astype(bf16), do_rcv, preferred_element_type=f32)

    grad_q = dq.reshape(rows, width).astype(bf16)
    grad_k = dk.reshape(rows, width).astype(bf16)
    grad_v = dv.reshape(rows, width).astype(bf16)
    grad_wq = dot_over_rows(normed_one, grad_q)
    grad_wk = dot_over_rows(normed_one, grad_k)
    grad_wv = dot_over_rows(normed_one, grad_v)
    grad_norm_one = dot_back(grad_q, full_query) + dot_back(grad_k, full_key) + dot_back(grad_v, full_value)
    norm_one_back = jax.vjp(layer_norm, in_rows, gain_first, shift_first)[1](grad_norm_one)
    grad_input = grad_middle + norm_one_back[0]

    shard_query = scatter_blocks(blocks_rows_cols(grad_wq, dp, tp))
    shard_key = scatter_blocks(blocks_rows_cols(grad_wk, dp, tp))
    shard_value = scatter_blocks(blocks_rows_cols(grad_wv, dp, tp))
    late_sums = summed_everywhere(
        [
            jnp.sum(grad_q, axis=0, dtype=f32),
            jnp.sum(grad_v, axis=0, dtype=f32),
            norm_one_back[1],
            norm_one_back[2],
        ]
    )
    vector_sums = (
        late_sums[0],
        late_sums[1],
        early_sums[0],
        early_sums[1],
        early_sums[2],
        late_sums[2],
        late_sums[3],
        early_sums[3],
        early_sums[4],
    )
    return (
        result,
        grad_input,
        shard_query,
        shard_key,
        shard_value,
        shard_out,
        shard_up,
        shard_down,
    ) + tuple(vector_sums)


def solution(mesh):
    rows_spec = P(("dp", "tensor"), None)
    placed = (
        rows_spec,
        P("dp"),
        rows_spec,
        P("dp", "tensor"),
        P("dp", "tensor"),
        P("dp", "tensor"),
        P("tensor", "dp"),
        P("dp", "tensor"),
        P("tensor", "dp"),
    ) + (P(),) * 9
    return jax.shard_map(
        body,
        mesh=mesh,
        in_specs=placed,
        out_specs=(
            rows_spec,
            rows_spec,
            P("dp", "tensor"),
            P("dp", "tensor"),
            P("dp", "tensor"),
            P("tensor", "dp"),
            P("dp", "tensor"),
            P("tensor", "dp"),
        )
        + (P(),) * 9,
        check_vma=False,
    )
```

time: 997 us -> 1240 us (1.24)
  local copies, waits for them, and re-layouts: 30.8 us -> 103 us
  blocking collectives: 80.2 us -> 144 us
  matrix products: 114 us -> 169 us
  waiting for transfers between devices: 692 us -> 742 us
  starting transfers between devices: 1.73 us -> 14.6 us
    reduce_scatter x6, waiting for transfers between devices: 345 us -> 466 us  [scatter_blocks(): return lax.psum_scatter(blocks, AXES, scatter_dimension=0, tiled=False)]
    unnamed x20 -> x12, waiting for transfers between devices: 118 us -> 4.91 us
    all_gather x4 -> x2, blocking collectives: 38.7 us -> 144 us  [summed_everywhere(): total = jnp.sum(lax.all_gather(joined, AXES, axis=0, tiled=False), axis=0)]
    reshape x6 -> x13, local copies, waits for them, and re-layouts: 6.47 us -> 63.9 us  [the longest x7 20.2 us: gather_rows_cols(): full.reshape(dp, tp, r, c).transpose(0, 2, 1, 3).reshape(dp * r, tp * c)]
    dot_general x12 -> x13, matrix products: 40.8 us -> 95.6 us  [the longest x1 20.5 us: body(): dp_oth = jnp.einsum('qhe,khe->hqk', do3, v_oth, preferred_element_type=f32)]
    psum x1 -> x0, blocking collectives: 41.5 us -> none  [body(): lax.psum((placed(column_sums[:head_width], b_query.shape[0], part_index),...]
    all_gather x6, waiting for transfers between devices: 230 us -> 251 us  [the longest x4 151 us: gather_rows_cols(): full = lax.all_gather(shard, AXES, axis=0, tiled=False)]
    ppermute x0 -> x6, waiting for transfers between devices: none -> 20.2 us  [the longest x2 20.2 us: body(): k_oth, v_oth = lax.ppermute((k3, v3), 'tensor', to_second)]
  transfers between devices with their start and end apart: 16 -> 18, of which waited for: 13 -> 11; matrix products, arithmetic and copies ran while one was open for 10% -> 25% of each run, Pallas kernels for 0% -> 0%
where the time goes in v1:
time: 1240 us; the launch traced here: 1230 us
  waiting for transfers between devices  742 us (60%)
  matrix products  169 us (14%)
  blocking collectives  144 us (12%)
  local copies, waits for them, and re-layouts  103 us (8%)
  other arithmetic  43.9 us (4%)
  between operations  15.3 us (1%)
  starting transfers between devices  14.6 us (1%)
    reduce_scatter x6, waiting for transfers between devices, scatter_blocks(): return lax.psum_scatter(blocks, AXES, scatter_dimension=0, tiled=False)  466 us
    all_gather x4, waiting for transfers between devices, gather_rows_cols(): full = lax.all_gather(shard, AXES, axis=0, tiled=False)  151 us
    all_gather x2, blocking collectives, summed_everywhere(): total = jnp.sum(lax.all_gather(joined, AXES, axis=0, tiled=False), axis=0)  144 us
    all_gather x2, waiting for transfers between devices, gather_cols_rows(): full = lax.all_gather(shard, AXES, axis=0, tiled=False)  100 us
    dot_general x6, matrix products, dot_right(): return jnp.dot(first_op, second_op, preferred_element_type=jnp.float32)  32.2 us
  transfers between devices with their start and end apart: 18, of which 11 were waited for; matrix products, arithmetic and copies ran while one was open for 25% of the time, Pallas kernels for 0%

profile of v1, /device:TPU:0, one launch (start us, length us, event | category | flops | bytes accessed | tf_op | source)
XLA Modules:
  0.0 1231.6 jit_solution(11448315027080163918)
XLA Ops:
  22.8 45.8 %all-gather.17.cloned.1.call-done = bf16[3072,192]{1,0:T(8,128)(2,1)} async-done(((bf16[96,192]{1,0:T(8,128)(2,1)}), bf16[3072,192]{1,0:T(8,128)(2,1)}) %all-gather.17.cloned.1.call-update) | async-done | bytes 1179664 | tf_op jit(solution)/shard_map/all_gather | solution.py:44
  72.8 52.6 %all-gather.19.cloned.1.call-done = bf16[3072,192]{1,0:T(8,128)(2,1)} async-done(((bf16[96,192]{1,0:T(8,128)(2,1)}), bf16[3072,192]{1,0:T(8,128)(2,1)}) %all-gather.19.cloned.1.call-update) | async-done | bytes 1179664 | tf_op jit(solution)/shard_map/all_gather | solution.py:44
  129.6 52.6 %all-gather.15.cloned.1.call-done = bf16[3072,192]{1,0:T(8,128)(2,1)} async-done(((bf16[96,192]{1,0:T(8,128)(2,1)}), bf16[3072,192]{1,0:T(8,128)(2,1)}) %all-gather.15.cloned.1.call-update) | async-done | bytes 1179664 | tf_op jit(solution)/shard_map/all_gather | solution.py:44
  188.1 50.8 %all-gather.21.cloned.1.call-done = bf16[6144,96]{1,0:T(8,128)(2,1)} async-done(((bf16[192,96]{1,0:T(8,128)(2,1)}), bf16[6144,96]{1,0:T(8,128)(2,1)}) %all-gather.21.cloned.1.call-update) | async-done | bytes 1179664 | tf_op jit(solution)/shard_map/all_gather | solution.py:50
  260.0 5.9 collective-permute-start.1
  269.1 9.9 collective-permute-done
  294.4 10.3 collective-permute-done.1
  311.9 6.3 fusion.75
  318.2 6.0 copy.150
  327.4 49.5 %all-gather.25.cloned.1.call-done = bf16[24576,96]{0,1:T(8,128)(2,1)} async-done(((bf16[768,96]{0,1:T(8,128)(2,1)}), bf16[24576,96]{0,1:T(8,128)(2,1)}) %all-gather.25.cloned.1.call-update) | async-done | bytes 4718608 | tf_op jit(solution)/shard_map/all_gather | solution.py:50
  376.9 7.5 reshape.421
  394.1 18.3 %multiply_convert_fusion.3 = (bf16[512,3072]{1,0:T(8,128)(2,1)S(1)}, f32[512,3072]{1,0:T(8,128)}, f32[512,3072]{1,0:T(8,128)}) fusion(f32[3072]{0:T(1024)S(1)} %convert_element_type.159, bf16[768,3072]{1,0:T(8,128)(2,1)S(1)} %bitcast.205, f32[512,768]{1,0:T(8,128)S(1)} %get-tuple-element.67, f32[768]{0:T(1024)S(1)} %convert_element_type.157, ...), kind=kOutput, calls=%fused_computation.25 | convolution fusion | flops 2521694208 | bytes 22042624 | tf_op jit(solution)/shard_map/dot_general | solution.py:24
  419.2 12.4 %reshape.423 = f32[4,768,8,96]{1,0,3,2:T(4,128)} reshape(f32[3072,768]{0,1:T(8,128)} %fusion.68) | data formatting | bytes 18874368 | tf_op jit(solution)/shard_map/reshape | solution.py:63
  431.6 8.9 copy.153
  440.6 8.2 convert_reduce_fusion
  448.7 6.1 fusion.70
  460.4 12.4 %reshape.425 = f32[8,96,4,768]{3,2,1,0:T(4,128)} reshape(f32[768,3072]{1,0:T(8,128)} %fusion.56) | data formatting | bytes 18874368 | tf_op jit(solution)/shard_map/reshape | solution.py:57
  472.8 9.0 copy.154
  499.6 9.2 fusion.6
  508.7 6.4 fusion.71
  515.2 20.5 %multiply_reduce_fusion = (f32[12,512]{1,0:T(8,128)S(1)}, f32[12,512]{1,0:T(8,128)S(1)}, f32[12,512,512]{1,2,0:T(8,128)}) fusion(f32[12,512,512]{1,2,0:T(8,128)} %copy-done, f32[12,512]{1,0:T(8,128)} %get-tuple-element.43, pred[512,512]{0,1:T(8,128)(4,1)S(1)} %get-tuple-element.60, f32[12,512,512]{1,2,0:T(8,128)} %fusion.71, f32[12,512,512]{1,2,0:T(8,128)} %copy-done.1, ...), kind=kOutput, calls=%fused_computation.4 | convolution fusion | flops 434098176 | bytes 52502528 | tf_op jit(solution)/shard_map/qhe,khe->hqk/dot_general | solution.py:202
  535.7 10.3 multiply_convert_fusion.2
  548.8 11.1 convert_reduce_fusion.4
  566.5 12.1 multiply_convert_fusion.6
  581.1 8.1 convert_reduce_fusion.3
  606.0 6.8 add_convert_fusion.2
  612.9 71.7 %all-gather.6 = f32[98304]{0:T(1024)S(1)} all-gather(f32[3072]{0:T(1024)S(1)} %pad_maximum_fusion), channel_id=8, replica_groups=mesh['dp'=8,'tensor'=4] {'dp','tensor'}, dimensions={0}, use_global_device_ids=true | all-gather | bytes 405504 | tf_op jit(solution)/shard_map/all_gather | solution.py:72
  684.8 72.1 %all-gather.7 = f32[196608]{0:T(1024)S(1)} all-gather(f32[6144]{0:T(1024)S(1)} %constant_dynamic-update-slice_fusion), channel_id=9, replica_groups=mesh['dp'=8,'tensor'=4] {'dp','tensor'}, dimensions={0}, use_global_device_ids=true | all-gather | bytes 811008 | tf_op jit(solution)/shard_map/all_gather | solution.py:72
  759.0 75.3 %reduce-scatter.9.cloned.1.call-done = f32[1,96,192]{2,1,0:T(8,128)} async-done(((f32[32,96,192]{2,1,0:T(8,128)}), f32[1,96,192]{2,1,0:T(8,128)}) %reduce-scatter.9.cloned.1.call-update) | async-done | bytes 73744 | tf_op jit(solution)/shard_map/reduce_scatter | solution.py:67
  834.3 107.1 %reduce-scatter.7.cloned.1.call-done = f32[1,96,192]{2,1,0:T(8,128)} async-done(((f32[32,96,192]{2,1,0:T(8,128)}), f32[1,96,192]{2,1,0:T(8,128)}) %reduce-scatter.7.cloned.1.call-update) | async-done | bytes 73744 | tf_op jit(solution)/shard_map/reduce_scatter | solution.py:67
  941.4 141.7 %reduce-scatter.17.cloned.1.call-done = f32[1,768,96]{1,2,0:T(8,128)} async-done(((f32[32,768,96]{1,2,0:T(8,128)}), f32[1,768,96]{1,2,0:T(8,128)}) %reduce-scatter.17.cloned.1.call-update) | async-done | bytes 294928 | tf_op jit(solution)/shard_map/reduce_scatter | solution.py:67
  1083.1 141.5 %reduce-scatter.15.cloned.1.call-done = f32[1,96,768]{2,1,0:T(8,128)} async-done(((f32[32,96,768]{2,1,0:T(8,128)}), f32[1,96,768]{2,1,0:T(8,128)}) %reduce-scatter.15.cloned.1.call-update) | async-done | bytes 294928 | tf_op jit(solution)/shard_map/reduce_scatter | solution.py:67
  (209 shorter events, 149.7 us)
Async XLA Ops:
  7.2 61.4 %all-gather.17.cloned.1.call-start = ((), (), s32[]{:S(2)}) async-start(), calls=%async_computation.13 | async-start | bytes 1622016 | tf_op jit(solution)/shard_map/all_gather | solution.py:44
  7.9 117.5 %all-gather.19.cloned.1.call-start = ((), (), s32[]{:S(2)}) async-start(), calls=%async_computation.14 | async-start | bytes 1622016 | tf_op jit(solution)/shard_map/all_gather | solution.py:44
  8.7 173.6 %all-gather.15.cloned.1.call-start = ((), (), s32[]{:S(2)}) async-start(), calls=%async_computation.12 | async-start | bytes 1622016 | tf_op jit(solution)/shard_map/all_gather | solution.py:44
  9.4 229.5 %all-gather.21.cloned.1.call-start = ((), (), s32[]{:S(2)}) async-start(), calls=%async_computation.15 | async-start | bytes 1622016 | tf_op jit(solution)/shard_map/all_gather | solution.py:50
  10.0 308.2 %all-gather.23.cloned.1.call-start = ((), (), s32[]{:S(2)}) async-start(), calls=%async_computation.16 | async-start | bytes 4866048 | tf_op jit(solution)/shard_map/all_gather | solution.py:44
  10.6 366.3 %all-gather.25.cloned.1.call-start = ((), (), s32[]{:S(2)}) async-start(), calls=%async_computation.17 | async-start | bytes 4866048 | tf_op jit(solution)/shard_map/all_gather | solution.py:50
  11.1 747.8 %reduce-scatter.13.cloned.1.call-start = ((), (), s32[]{:S(2)}) async-start(), calls=%async_computation.9 | async-start | bytes 3244032 | tf_op jit(solution)/shard_map/reduce_scatter | solution.py:67
  14.4 238.8 %copy-start.29 = (f32[512]{0:T(512)}, f32[512]{0:T(512)S(1)}, u32[]{:S(2)}) copy-start(f32[512]{0:T(512)S(1)} %broadcast_multiply_fusion.1) | copy-start | bytes 6148
  16.0 237.3 %copy-start.31 = (f32[512]{0:T(512)}, f32[512]{0:T(512)S(1)}, u32[]{:S(2)}) copy-start(f32[512]{0:T(512)S(1)} %fusion.41) | copy-start | bytes 6148
  16.7 236.6 %copy-start.27 = (f32[768]{0:T(1024)}, f32[768]{0:T(1024)S(1)}, u32[]{:S(2)}) copy-start(f32[768]{0:T(1024)S(1)} %convert_element_type.142) | copy-start | bytes 9220
  17.4 235.9 %copy-start.35 = (f32[768]{0:T(1024)}, f32[768]{0:T(1024)S(1)}, u32[]{:S(2)}) copy-start(f32[768]{0:T(1024)S(1)} %convert_element_type.143) | copy-start | bytes 9220
  22.8 267.1 %copy-start.9 = (pred[512,512]{0,1:T(8,128)(4,1)}, pred[512,512]{0,1:T(8,128)(4,1)S(1)}, u32[]{:S(2)}) copy-start(pred[512,512]{0,1:T(8,128)(4,1)S(1)} %get-tuple-element.61) | copy-start | bytes 786436
  185.0 61.2 %copy-start.2 = (bf16[512,768]{1,0:T(8,128)(2,1)S(1)}, bf16[512,768]{1,0:T(8,128)(2,1)}, u32[]{:S(2)}) copy-start(bf16[512,768]{1,0:T(8,128)(2,1)} %param.18) | copy-start | bytes 2359300
  188.1 59.1 %copy-start.10 = (bf16[768,768]{0,1:T(8,128)(2,1)}, bf16[768,768]{0,1:T(8,128)(2,1)S(1)}, u32[]{:S(2)}) copy-start(bf16[768,768]{0,1:T(8,128)(2,1)S(1)} %reshape.409) | copy-start | bytes 3538948
  250.9 28.2 %collective-permute-start = (bf16[512,12,64]{0,2,1:T(8,128)(2,1)S(1)}, bf16[512,12,64]{0,2,1:T(8,128)(2,1)S(1)}, u32[]{:S(2)}, u32[]{:S(2)}) collective-permute-start(bf16[512,12,64]{0,2,1:T(8,128)(2,1)S(1)} %bitcast.182), channel_id=1, source_target_pairs={{0,1},{2,3},{4,5},{6,7},{8,9},{10,11},{12,13},{14,15},{16,17},{18,... | collective-permute-start | bytes 2359304 | tf_op jit(solution)/shard_map/ppermute | solution.py:147
  258.7 52.3 %collective-permute-start.2 = (bf16[512,12,64]{0,2,1:T(8,128)(2,1)}, bf16[512,12,64]{0,2,1:T(8,128)(2,1)S(1)}, u32[]{:S(2)}, u32[]{:S(2)}) collective-permute-start(bf16[512,12,64]{0,2,1:T(8,128)(2,1)} %bitcast.6), channel_id=1, source_target_pairs={{1,0},{3,2},{5,4},{7,6},{9,8},{11,10},{13,12},{15,14},{17,16},{19,... | collective-permute-start | bytes 2359304 | tf_op jit(solution)/shard_map/ppermute | solution.py:162
  260.0 44.7 %collective-permute-start.1 = (bf16[512,12,64]{0,2,1:T(8,128)(2,1)}, bf16[512,12,64]{0,2,1:T(8,128)(2,1)}, u32[]{:S(2)}, u32[]{:S(2)}) collective-permute-start(bf16[512,12,64]{0,2,1:T(8,128)(2,1)} %bitcast.206), channel_id=1, source_target_pairs={{0,1},{2,3},{4,5},{6,7},{8,9},{10,11},{12,13},{14,15},{16,17},{18,... | collective-permute-start | bytes 2359304 | tf_op jit(solution)/shard_map/ppermute | solution.py:147
  269.1 20.9 %copy-start.1 = (f32[12,512,512]{1,2,0:T(8,128)}, f32[12,512,512]{1,2,0:T(8,128)S(1)}, u32[]{:S(2)}) copy-start(f32[12,512,512]{1,2,0:T(8,128)S(1)} %get-tuple-element.63) | copy-start | bytes 37748740
  282.5 22.1 %copy-start = (f32[12,512,512]{1,2,0:T(8,128)}, f32[12,512,512]{1,2,0:T(8,128)S(1)}, u32[]{:S(2)}) copy-start(f32[12,512,512]{1,2,0:T(8,128)S(1)} %get-tuple-element.65) | copy-start | bytes 37748740
  288.7 277.8 %collective-permute-start.3 = (f32[12,512,1]{1,0,2:T(8,128)}, f32[12,512,1]{1,0,2:T(8,128)}, u32[]{:S(2)}, u32[]{:S(2)}) collective-permute-start(f32[12,512,1]{1,0,2:T(8,128)} %bitcast.34), channel_id=1, source_target_pairs={{1,0},{3,2},{5,4},{7,6},{9,8},{11,10},{13,12},{15,14},{17,16},{19,... | collective-permute-start | bytes 73736 | tf_op jit(solution)/shard_map/ppermute | solution.py:162
  294.4 15.3 %copy-start.22 = (bf16[768,768]{1,0:T(8,128)(2,1)S(1)}, bf16[768,768]{1,0:T(8,128)(2,1)}, u32[]{:S(2)}) copy-start(bf16[768,768]{1,0:T(8,128)(2,1)} %reshape.418) | copy-start | bytes 3538948
  497.7 11.0 copy-start.8
  497.7 11.0 copy-start.15
  497.7 68.8 %collective-permute-start.4 = (bf16[512,12,64]{0,2,1:T(8,128)(2,1)}, bf16[512,12,64]{0,2,1:T(8,128)(2,1)}, u32[]{:S(2)}, u32[]{:S(2)}) collective-permute-start(bf16[512,12,64]{0,2,1:T(8,128)(2,1)} %bitcast.193), channel_id=1, source_target_pairs={{1,0},{3,2},{5,4},{7,6},{9,8},{11,10},{13,12},{15,14},{17,16},{19,... | collective-permute-start | bytes 2359304 | tf_op jit(solution)/shard_map/ppermute | solution.py:206
  515.2 243.8 %reduce-scatter.11.cloned.1.call-start = ((), (), s32[]{:S(2)}) async-start(), calls=%async_computation.8 | async-start | bytes 3244032 | tf_op jit(solution)/shard_map/reduce_scatter | solution.py:67
  546.1 20.4 %collective-permute-start.5 = (f32[12,512,1]{1,0,2:T(8,128)S(1)}, f32[12,512,1]{1,0,2:T(8,128)S(1)}, u32[]{:S(2)}, u32[]{:S(2)}) collective-permute-start(f32[12,512,1]{1,0,2:T(8,128)S(1)} %bitcast.223), channel_id=1, source_target_pairs={{1,0},{3,2},{5,4},{7,6},{9,8},{11,10},{13,12},{15,14},{17,16},{19,... | collective-permute-start | bytes 73736 | tf_op jit(solution)/shard_map/ppermute | solution.py:206
  581.1 8.2 copy-start.3
  581.1 8.2 copy-start.11
  597.8 236.4 %reduce-scatter.9.cloned.1.call-start = ((), (), s32[]{:S(2)}) async-start(), calls=%async_computation.7 | async-start | bytes 3244032 | tf_op jit(solution)/shard_map/reduce_scatter | solution.py:67
  601.8 339.6 %reduce-scatter.7.cloned.1.call-start = ((), (), s32[]{:S(2)}) async-start(), calls=%async_computation.6 | async-start | bytes 3244032 | tf_op jit(solution)/shard_map/reduce_scatter | solution.py:67
  604.5 478.5 %reduce-scatter.17.cloned.1.call-start = ((), (), s32[]{:S(2)}) async-start(), calls=%async_computation.11 | async-start | bytes 9732096 | tf_op jit(solution)/shard_map/reduce_scatter | solution.py:67
  605.3 619.2 %reduce-scatter.15.cloned.1.call-start = ((), (), s32[]{:S(2)}) async-start(), calls=%async_computation.10 | async-start | bytes 9732096 | tf_op jit(solution)/shard_map/reduce_scatter | solution.py:67
  (28 other events, 101.6 us)
Sparse Core Ops, SparseCore 0:
  10.9 57.6 all-gather.16
  71.5 53.8 all-gather.18
  128.3 53.8 all-gather.14
  185.0 53.8 all-gather.20
  241.5 68.5 all-gather.22
  312.8 64.0 all-gather.24
  515.3 103.2 reduce-scatter.12
  624.6 102.2 reduce-scatter.10
  732.9 101.3 reduce-scatter.8
  840.1 101.1 reduce-scatter.6
  947.8 135.2 reduce-scatter.16
  1089.4 135.0 reduce-scatter.14

commit v2 on v1

--- a/solution.py
+++ b/solution.py
@@ -3,6 +3,7 @@
 from jax import lax
 from jax.sharding import PartitionSpec as P
 
+
 HEAD = 64
 SEQ_LEN = 1024
 
@@ -39,42 +40,37 @@
 AXES = ("dp", "tensor")
 
 
-def gather_rows_cols(shard, dp, tp):
-    r, c = shard.shape
-    full = lax.all_gather(shard, AXES, axis=0, tiled=False)
-    return full.reshape(dp, tp, r, c).transpose(0, 2, 1, 3).reshape(dp * r, tp * c)
-
-
-def gather_cols_rows(shard, dp, tp):
-    r, c = shard.shape
-    full = lax.all_gather(shard, AXES, axis=0, tiled=False)
-    return full.reshape(dp, tp, r, c).transpose(1, 2, 0, 3).reshape(tp * r, dp * c)
-
-
-def blocks_rows_cols(grad, dp, tp):
-    rows, cols = grad.shape
-    r, c = rows // dp, cols // tp
-    return grad.reshape(dp, r, tp, c).transpose(0, 2, 1, 3).reshape(dp * tp, r, c)
-
-
-def blocks_cols_rows(grad, dp, tp):
-    rows, cols = grad.shape
-    r, c = rows // tp, cols // dp
-    return grad.reshape(tp, r, dp, c).transpose(2, 0, 1, 3).reshape(dp * tp, r, c)
-
-
-def scatter_blocks(blocks):
-    return lax.psum_scatter(blocks, AXES, scatter_dimension=0, tiled=False)
-
-
-def summed_everywhere(vectors):
-    joined = jnp.concatenate(vectors)
-    total = jnp.sum(lax.all_gather(joined, AXES, axis=0, tiled=False), axis=0)
+def gather_joined(shards, dp, tp):
+    r = shards[0].shape[0]
+    joined = jnp.concatenate(shards, axis=1)
+    full = lax.all_gather(joined, AXES, axis=0, tiled=False).reshape(dp, tp, r, -1)
     out = []
     start = 0
-    for v in vectors:
-        out.append(total[start : start + v.shape[0]])
-        start += v.shape[0]
+    for piece in shards:
+        c = piece.shape[1]
+        block = full[:, :, :, start : start + c]
+        out.append(block.transpose(0, 2, 1, 3).reshape(dp * r, tp * c))
+        start += c
+    return out
+
+
+def scatter_rows(grad):
+    return lax.psum_scatter(grad, "dp", scatter_dimension=0, tiled=True)
+
+
+def scatter_cols_joined(pieces, tp):
+    parts = []
+    for piece in pieces:
+        r, c = piece.shape
+        parts.append(piece.reshape(r, tp, c // tp).transpose(1, 0, 2))
+    joined = jnp.concatenate(parts, axis=2)
+    mine = lax.psum_scatter(joined, "tensor", scatter_dimension=0, tiled=False)
+    out = []
+    start = 0
+    for piece in pieces:
+        c = piece.shape[1] // tp
+        out.append(mine[:, start : start + c])
+        start += c
     return out
 
 
@@ -85,7 +81,7 @@
     return jnp.where(visible[None], scores, masked_score)
 
 
-def body(
+def layer(
     inputs,
     prefix,
     cotangent,
@@ -121,12 +117,10 @@
     to_second = [(t, t + 1) for t in range(0, tp, 2)]
     to_first = [(t + 1, t) for t in range(0, tp, 2)]
 
-    full_query = gather_rows_cols(w_query, dp, tp)
-    full_key = gather_rows_cols(w_key, dp, tp)
-    full_value = gather_rows_cols(w_value, dp, tp)
-    full_out = gather_cols_rows(w_out, dp, tp)
-    full_up = gather_rows_cols(w_up, dp, tp)
-    full_down = gather_cols_rows(w_down, dp, tp)
+    full_query, full_key, full_value, out_t = gather_joined([w_query, w_key, w_value, w_out.T], dp, tp)
+    full_out = out_t.T
+    full_up, down_t = gather_joined([w_up, w_down.T], dp, tp)
+    full_down = down_t.T
     width = full_query.shape[1]
     heads = width // HEAD
 
@@ -168,31 +162,22 @@
     result = (middle + dot_right(activated, full_down) + b_down.astype(f32)).astype(bf16)
 
     grad_result = cotangent.astype(f32)
-    down_blocks = blocks_cols_rows(dot_over_rows(activated, cotangent), dp, tp)
+    down_t_grad = dot_over_rows(cotangent, activated)
     grad_act = dot_back(cotangent, full_down)
-    down_blocks, grad_act = lax.optimization_barrier((down_blocks, grad_act))
-    shard_down = scatter_blocks(down_blocks)
+    down_t_grad, grad_act = lax.optimization_barrier((down_t_grad, grad_act))
+    down_rows = scatter_rows(down_t_grad)
     grad_pre = jax.vjp(gelu_exact, pre_act)[1](grad_act)[0].astype(bf16)
-    up_blocks = blocks_rows_cols(dot_over_rows(normed_two, grad_pre), dp, tp)
+    up_grad = dot_over_rows(normed_two, grad_pre)
     grad_norm_two = dot_back(grad_pre, full_up)
-    up_blocks, grad_norm_two = lax.optimization_barrier((up_blocks, grad_norm_two))
-    shard_up = scatter_blocks(up_blocks)
+    up_grad, grad_norm_two = lax.optimization_barrier((up_grad, grad_norm_two))
+    up_rows = scatter_rows(up_grad)
     norm_two_back = jax.vjp(layer_norm, middle, gain_second, shift_second)[1](grad_norm_two)
     grad_middle = grad_result + norm_two_back[0]
-    early_sums = summed_everywhere(
-        [
-            jnp.sum(grad_middle, axis=0),
-            jnp.sum(grad_pre, axis=0, dtype=f32),
-            jnp.sum(grad_result, axis=0),
-            norm_two_back[1],
-            norm_two_back[2],
-        ]
-    )
     grad_attn_rows = grad_middle.astype(bf16)
-    out_blocks = blocks_cols_rows(dot_over_rows(attended, grad_attn_rows), dp, tp)
+    out_t_grad = dot_over_rows(grad_attn_rows, attended)
     grad_attended = dot_back(grad_attn_rows, full_out).astype(bf16)
-    out_blocks, grad_attended = lax.optimization_barrier((out_blocks, grad_attended))
-    shard_out = scatter_blocks(out_blocks)
+    out_t_grad, grad_attended = lax.optimization_barrier((out_t_grad, grad_attended))
+    out_rows = scatter_rows(out_t_grad)
     do3 = grad_attended.reshape(shape3)
 
     scaling = HEAD ** (-0.5)
@@ -222,34 +207,31 @@
     grad_q = dq.reshape(rows, width).astype(bf16)
     grad_k = dk.reshape(rows, width).astype(bf16)
     grad_v = dv.reshape(rows, width).astype(bf16)
-    grad_wq = dot_over_rows(normed_one, grad_q)
-    grad_wk = dot_over_rows(normed_one, grad_k)
-    grad_wv = dot_over_rows(normed_one, grad_v)
+    grad_qkv = jnp.concatenate([grad_q, grad_k, grad_v], axis=1)
+    qkv_rows = scatter_rows(dot_over_rows(normed_one, grad_qkv))
     grad_norm_one = dot_back(grad_q, full_query) + dot_back(grad_k, full_key) + dot_back(grad_v, full_value)
     norm_one_back = jax.vjp(layer_norm, in_rows, gain_first, shift_first)[1](grad_norm_one)
     grad_input = grad_middle + norm_one_back[0]
 
-    shard_query = scatter_blocks(blocks_rows_cols(grad_wq, dp, tp))
-    shard_key = scatter_blocks(blocks_rows_cols(grad_wk, dp, tp))
-    shard_value = scatter_blocks(blocks_rows_cols(grad_wv, dp, tp))
-    late_sums = summed_everywhere(
-        [
+    shard_query, shard_key, shard_value, shard_out_t, shard_up, shard_down_t = scatter_cols_joined(
+        [qkv_rows[:, :width], qkv_rows[:, width : 2 * width], qkv_rows[:, 2 * width :], out_rows, up_rows, down_rows],
+        tp,
+    )
+    shard_out = shard_out_t.T
+    shard_down = shard_down_t.T
+    vector_sums = lax.psum(
+        (
             jnp.sum(grad_q, axis=0, dtype=f32),
             jnp.sum(grad_v, axis=0, dtype=f32),
+            jnp.sum(grad_middle, axis=0),
+            jnp.sum(grad_pre, axis=0, dtype=f32),
+            jnp.sum(grad_result, axis=0),
             norm_one_back[1],
             norm_one_back[2],
-        ]
-    )
-    vector_sums = (
-        late_sums[0],
-        late_sums[1],
-        early_sums[0],
-        early_sums[1],
-        early_sums[2],
-        late_sums[2],
-        late_sums[3],
-        early_sums[3],
-        early_sums[4],
+            norm_two_back[1],
+            norm_two_back[2],
+        ),
+        AXES,
     )
     return (
         result,
@@ -277,7 +259,7 @@
         P("tensor", "dp"),
     ) + (P(),) * 9
     return jax.shard_map(
-        body,
+        layer,
         mesh=mesh,
         in_specs=placed,
         out_specs=(

time: 1240 us -> 675 us (0.54)
  waiting for transfers between devices: 742 us -> 282 us
  blocking collectives: 144 us -> 43.6 us
    reduce_scatter x6 -> x4, waiting for transfers between devices: 466 us -> 135 us  [the longest x3 129 us: scatter_rows(): return lax.psum_scatter(grad, 'dp', scatter_dimension=0, tiled=True)]
    all_gather x6 -> x2, waiting for transfers between devices: 251 us -> 54.4 us  [gather_joined(): lax.all_gather(joined, AXES, axis=0, tiled=False).reshape(dp, tp, r, -1)]
    all_gather x2 -> x0, blocking collectives: 144 us -> none  [summed_everywhere(): total = jnp.sum(lax.all_gather(joined, AXES, axis=0, tiled=False), axis=0)]
    unnamed x12 -> x8, waiting for transfers between devices: 4.91 us -> 78.4 us
    psum x0 -> x1, blocking collectives: none -> 43.6 us  [layer(): lax.psum((jnp.sum(grad_q, axis=0, dtype=f32), jnp.sum(grad_v, axis=0, dty...]
    reshape x13 -> x14, local copies, waits for them, and re-layouts: 63.9 us -> 34.4 us  [the longest x10 20 us: scatter_cols_joined(): parts.append(piece.reshape(r, tp, c // tp).transpose(1, 0, 2))]
    unnamed x90 -> x106, local copies, waits for them, and re-layouts: 7.11 us -> 26.5 us
  transfers between devices with their start and end apart: 18 -> 13, of which waited for: 11 -> 6; matrix products, arithmetic and copies ran while one was open for 25% -> 43% of each run, Pallas kernels for 0% -> 0%
where the time goes in v2:
time: 675 us; the launch traced here: 664 us
  waiting for transfers between devices  282 us (42%)
  matrix products  164 us (24%)
  local copies, waits for them, and re-layouts  101 us (15%)
  blocking collectives  43.6 us (6%)
  other arithmetic  42.4 us (6%)
  starting transfers between devices  15.8 us (2%)
  between operations  15.4 us (2%)
    reduce_scatter x3, waiting for transfers between devices, scatter_rows(): return lax.psum_scatter(grad, 'dp', scatter_dimension=0, tiled=True)  129 us
    unnamed x8, waiting for transfers between devices  78.4 us
    all_gather x2, waiting for transfers between devices, gather_joined(): lax.all_gather(joined, AXES, axis=0, tiled=False).reshape(dp, tp, r, -1)  54.4 us
    psum x1, blocking collectives, layer(): lax.psum((jnp.sum(grad_q, axis=0, dtype=f32), jnp.sum(grad_v, axis=0, dty...  43.6 us
    dot_general x6, matrix products, dot_right(): return jnp.dot(first_op, second_op, preferred_element_type=jnp.float32)  31.4 us
    unnamed x106, local copies, waits for them, and re-layouts  26.5 us
    dot_general x4, matrix products, dot_over_rows(): lax.dot_general(first_op, second_op, (((0,), (0,)), ((), ())), preferred_...  20.2 us
    dot_general x1, matrix products, layer(): dp_oth = jnp.einsum('qhe,khe->hqk', do3, v_oth, preferred_element_type=f32)  20 us
  transfers between devices with their start and end apart: 13, of which 6 were waited for; matrix products, arithmetic and copies ran while one was open for 43% of the time, Pallas kernels for 0%

profile of v2, /device:TPU:0, one launch (start us, length us, event | category | flops | bytes accessed | tf_op | source)
XLA Modules:
  0.0 663.9 jit_solution(12076780029748328794)
XLA Ops:
  23.3 54.4 %all-gather.5.cloned.1.call-done = bf16[3072,768]{1,0:T(8,128)(2,1)} async-done(((bf16[96,768]{1,0:T(8,128)(2,1)}), bf16[3072,768]{1,0:T(8,128)(2,1)}) %all-gather.5.cloned.1.call-update) | async-done | bytes 4718608 | tf_op jit(solution)/shard_map/all_gather | solution.py:46
  77.7 7.0 %slice_bitcast_fusion = (bf16[8,96,4,192]{3,1,2,0:T(8,128)(2,1)}, bf16[8,96,4,192]{3,1,2,0:T(8,128)(2,1)S(1)}, bf16[8,96,4,192]{3,1,2,0:T(8,128)(2,1)}, bf16[8,96,4,192]{3,1,2,0:T(8,128)(2,1)}) fusion(bf16[8,4,96,768]{3,2,1,0:T(8,128)(2,1)} %bitcast.150), kind=kLoop, calls=%fused_computation.76 | loop fusion | bytes 9437184 | tf_op jit(solution)/shard_map/transpose | solution.py:52
  87.6 3.9 reshape.385
  100.5 4.2 collective-permute-start
  129.2 5.7 collective-permute-start.1
  137.0 3.9 fusion.4
  140.9 5.5 fusion.1
  148.3 4.4 fusion.21
  152.7 14.1 %collective-permute-done.1 = bf16[512,12,64]{0,2,1:T(8,128)(2,1)S(1)} collective-permute-done((bf16[512,12,64]{0,2,1:T(8,128)(2,1)}, bf16[512,12,64]{0,2,1:T(8,128)(2,1)S(1)}, u32[]{:S(2)}, u32[]{:S(2)}) %collective-permute-start.1) | collective-permute-done | bytes 786464 | tf_op jit(solution)/shard_map/ppermute | solution.py:141
  166.8 5.5 add_convert_fusion.4
  174.8 7.5 %fusion.83 = f32[12,512,512]{1,2,0:T(8,128)} fusion(bf16[512,12,64]{0,2,1:T(8,128)(2,1)} %collective-permute-done.2, bf16[512,12,64]{0,2,1:T(8,128)(2,1)S(1)} %bitcast.143), kind=kOutput, calls=%fused_computation.154 | convolution fusion | flops 402653184 | bytes 14155776 | tf_op jit(solution)/shard_map/qhe,khe->hqk/dot_general | solution.py:79
  182.3 4.6 fusion.75
  199.2 16.0 %multiply_convert_fusion.3 = (bf16[512,3072]{1,0:T(8,128)(2,1)S(1)}, f32[512,3072]{1,0:T(8,128)S(1)}, f32[512,3072]{1,0:T(8,128)S(1)}) fusion(f32[3072]{0:T(1024)S(1)} %convert_element_type.159, bf16[768,3072]{1,0:T(8,128)(2,1)S(1)} %bitcast.157, f32[512,768]{1,0:T(8,128)S(1)} %copy-done.10, f32[768]{0:T(1024)S(1)} %convert_element_type.157, ...), kind=kOutput, calls=%fused_computation.25 | convolution fusion | flops 2521694208 | bytes 22042624 | tf_op jit(solution)/shard_map/dot_general | solution.py:25
  215.3 5.2 convolution_bitcast_fusion
  224.2 3.8 fusion.78
  228.0 5.9 fusion.65
  245.6 7.4 %fusion.79 = f32[12,512,512]{1,2,0:T(8,128)} fusion(bf16[512,12,64]{0,2,1:T(8,128)(2,1)S(1)} %bitcast.152, bf16[512,12,64]{0,2,1:T(8,128)(2,1)} %bitcast.161), kind=kOutput, calls=%fused_computation.150 | convolution fusion | flops 402653184 | bytes 14155776 | tf_op jit(solution)/shard_map/qhe,khe->hqk/dot_general | solution.py:186
  253.1 20.0 %multiply_reduce_fusion = (f32[12,512]{1,0:T(8,128)S(1)}, f32[12,512]{1,0:T(8,128)S(1)}, f32[12,512,512]{1,2,0:T(8,128)}) fusion(f32[12,512,512]{1,2,0:T(8,128)} %copy-done.1, f32[12,512]{1,0:T(8,128)} %get-tuple-element.104, pred[512,512]{0,1:T(8,128)(4,1)} %copy-done.16, f32[12,512,512]{1,2,0:T(8,128)} %fusion.79, f32[12,512,512]{1,2,0:T(8,128)} %copy-done, ...), kind=kOutput, calls=%fused_computation.4 | convolution fusion | flops 434098176 | bytes 52502528 | tf_op jit(solution)/shard_map/qhe,khe->hqk/dot_general | solution.py:187
  273.1 10.3 %multiply_convert_fusion.2 = bf16[12,512,512]{1,2,0:T(8,128)(2,1)S(1)} fusion(f32[12,512,512]{1,2,0:T(8,128)} %fusion.79, f32[12,512]{1,0:T(8,128)S(1)} %add.257, f32[12,512]{1,0:T(8,128)} %get-tuple-element.104, f32[12,512,512]{1,2,0:T(8,128)} %copy-done, pred[512,512]{0,1:T(8,128)(4,1)S(1)} %get-tuple-element.128), kind=kLoop, calls=%fused_computation.3 | loop fusion | flops 18874368 | bytes 31768576 | tf_op jit(solution)/shard_map/convert_element_type | solution.py:192
  286.5 14.4 %convert_reduce_fusion.4 = (f32[12,64]{1,0:T(8,128)S(1)}, bf16[12,64,512]{2,1,0:T(8,128)(2,1)}) fusion(f32[12,64,512]{2,1,0:T(8,128)S(1)} %fusion.80, bf16[512,12,64]{0,2,1:T(8,128)(2,1)} %collective-permute-done, f32[12,512,512]{1,2,0:T(8,128)} %get-tuple-element.136, f32[12,512,512]{1,2,0:T(8,128)} %copy-done.1, f32[12,512]{1,0:T(8,128)S(1)} %add.257, ...), kind=kOutput, calls=%fused_computation.82 | convolution fusion | flops 423492864 | bytes 28625920 | tf_op jit(solution)/shard_map/hqk,khe->qhe/dot_general | solution.py:196
  300.9 4.2 fusion.6
  308.3 9.3 %convert_reduce_fusion.3 = (f32[12,64]{1,0:T(8,128)}, bf16[12,64,512]{2,1,0:T(8,128)(2,1)}) fusion(f32[12,64,512]{2,1,0:T(8,128)S(1)} %fusion.6, bf16[512,12,64]{0,2,1:T(8,128)(2,1)} %collective-permute-done.4, f32[12,512,512]{1,2,0:T(8,128)} %fusion.83, f32[12,512]{1,0:T(8,128)} %bitcast.23, pred[512,512]{0,1:T(8,128)(4,1)S(1)} %copy-done.26), kind=kOutput, calls=%fused_computation.81 | convolution fusion | flops 416808192 | bytes 16018432 | tf_op jit(solution)/shard_map/hqk,qhe->khe/dot_general | solution.py:205
  317.7 12.5 %multiply_convert_fusion.6 = bf16[12,64,512]{2,1,0:T(8,128)(2,1)} fusion(f32[12,64,512]{2,1,0:T(8,128)} %fusion.82, bf16[512,12,64]{0,2,1:T(8,128)(2,1)} %collective-permute-done.2, f32[12,512,512]{1,2,0:T(8,128)} %fusion.83, f32[12,512]{1,0:T(8,128)S(1)} %bitcast.180, f32[12,512]{1,0:T(8,128)} %bitcast.23, pred[512,512]{0,1:T(8,128)(4,1)S(1)} %copy-done.26, ...), kind=kOutput, calls=%fused_computation.86 | convolution fusion | flops 825360384 | bytes 17612800 | tf_op jit(solution)/shard_map/hqk,qhe->khe/dot_general | solution.py:204
  330.3 6.8 %fusion.30 = f32[768,2304]{1,0:T(8,128)} fusion(bf16[512,768]{0,1:T(8,128)(2,1)} %bitcast.173, bf16[512,768]{0,1:T(8,128)(2,1)} %bitcast.181, bf16[512,768]{0,1:T(8,128)(2,1)} %bitcast.175, bf16[512,768]{1,0:T(8,128)(2,1)S(1)} %copy-done.5, f32[768]{0:T(1024)S(1)} %copy-done.43, f32[768]{0:T(1024)S(1)} %copy-done.28, f32[512]{0:T(512)S(1)} %copy-done.35, ...), kind=kOutput, calls=%fused_computation.60 | convolution fusion | flops 1821376512 | bytes 10233856 | tf_op jit(solution)/shard_map/dot_general | solution.py:35
  337.7 9.7 %copy.138 = f32[768,3072]{1,0:T(8,128)} copy(f32[768,3072]{0,1:T(8,128)} %convolution_bitcast_fusion) | data formatting | bytes 18874368
  350.8 63.0 %reduce-scatter.8.cloned.1.call-done = f32[96,2304]{1,0:T(8,128)} async-done(((f32[768,2304]{1,0:T(8,128)}), f32[96,2304]{1,0:T(8,128)}) %reduce-scatter.8.cloned.1.call-update) | async-done | bytes 884752 | tf_op jit(solution)/shard_map/reduce_scatter | solution.py:58
  427.5 66.5 %reduce-scatter.12.cloned.1.call-done = f32[96,3072]{1,0:T(8,128)} async-done(((f32[768,3072]{1,0:T(8,128)}), f32[96,3072]{1,0:T(8,128)}) %reduce-scatter.12.cloned.1.call-update) | async-done | bytes 1179664 | tf_op jit(solution)/shard_map/reduce_scatter | solution.py:58
  496.3 77.8 %reduce-scatter.16.cloned.1.call-done = f32[96,3072]{1,0:T(8,128)} async-done(((f32[768,3072]{1,0:T(8,128)}), f32[96,3072]{1,0:T(8,128)}) %reduce-scatter.16.cloned.1.call-update) | async-done | bytes 1179664
  579.9 4.5 concatenate.15
  588.8 6.5 add_convert_fusion.2
  603.4 43.6 %all-reduce = (f32[768]{0:T(1024)}, f32[768]{0:T(1024)}, f32[768]{0:T(1024)}, f32[3072]{0:T(1024)}, f32[768]{0:T(1024)}, /*index=5*/f32[768]{0:T(1024)}, f32[768]{0:T(1024)}, f32[768]{0:T(1024)}, f32[768]{0:T(1024)}) all-reduce(f32[768]{0:T(1024)S(1)} %reduce_sum.212, ...), channel_id=1, replica_groups=mesh['dp'=8,'tensor'=4] {'dp','tensor'}, use_global_device_ids=true, to_apply=%region_20.21 | all-reduce | flops 9216 | bytes 73728 | tf_op jit(solution)/shard_map/psum | solution.py:222
  647.0 5.2 reduce-scatter.14.cloned.1.call-done
  (204 shorter events, 135.3 us)
Async XLA Ops:
  7.2 70.5 %all-gather.5.cloned.1.call-start = ((), (), s32[]{:S(2)}) async-start(), calls=%async_computation.9 | async-start | bytes 4866048 | tf_op jit(solution)/shard_map/all_gather | solution.py:46
  9.8 172.5 %all-gather.7.cloned.1.call-start = ((), (), s32[]{:S(2)}) async-start(), calls=%async_computation.10 | async-start | bytes 9732096 | tf_op jit(solution)/shard_map/all_gather | solution.py:46
  11.6 336.1 %reduce-scatter.10.cloned.1.call-start = ((), (), s32[]{:S(2)}) async-start(), calls=%async_computation.6 | async-start | bytes 2654208 | tf_op jit(solution)/shard_map/reduce_scatter | solution.py:58
  12.3 111.4 %copy-start.27 = (f32[768]{0:T(1024)}, f32[768]{0:T(1024)S(1)}, u32[]{:S(2)}) copy-start(f32[768]{0:T(1024)S(1)} %convert_element_type.142) | copy-start | bytes 9220
  13.0 110.7 %copy-start.42 = (f32[768]{0:T(1024)}, f32[768]{0:T(1024)S(1)}, u32[]{:S(2)}) copy-start(f32[768]{0:T(1024)S(1)} %convert_element_type.143) | copy-start | bytes 9220
  20.4 103.4 %copy-start.29 = (f32[512]{0:T(512)}, f32[512]{0:T(512)S(1)}, u32[]{:S(2)}) copy-start(f32[512]{0:T(512)S(1)} %broadcast_multiply_fusion.1) | copy-start | bytes 6148
  21.9 62.8 %copy-start.37 = (f32[512]{0:T(512)}, f32[512]{0:T(512)S(1)}, u32[]{:S(2)}) copy-start(f32[512]{0:T(512)S(1)} %fusion.41) | copy-start | bytes 6148
  21.9 101.9 %copy-start.34 = (f32[512]{0:T(512)}, f32[512]{0:T(512)S(1)}, u32[]{:S(2)}) copy-start(f32[512]{0:T(512)S(1)} %fusion.49) | copy-start | bytes 6148
  23.3 143.5 %copy-start.16 = (pred[512,512]{0,1:T(8,128)(4,1)}, pred[512,512]{0,1:T(8,128)(4,1)S(1)}, u32[]{:S(2)}) copy-start(pred[512,512]{0,1:T(8,128)(4,1)S(1)} %get-tuple-element.127) | copy-start | bytes 786436
  100.5 74.3 %copy-start.7 = (bf16[512,768]{0,1:T(8,128)(2,1)}, bf16[512,768]{0,1:T(8,128)(2,1)S(1)}, u32[]{:S(2)}) copy-start(bf16[512,768]{0,1:T(8,128)(2,1)S(1)} %copy.104) | copy-start | bytes 2359300
  100.5 36.5 %collective-permute-start = (bf16[512,12,64]{0,2,1:T(8,128)(2,1)S(1)}, bf16[512,12,64]{0,2,1:T(8,128)(2,1)}, u32[]{:S(2)}, u32[]{:S(2)}) collective-permute-start(bf16[512,12,64]{0,2,1:T(8,128)(2,1)S(1)} %bitcast.141), channel_id=1, source_target_pairs={{0,1},{2,3},{4,5},{6,7},{8,9},{10,11},{12,13},{14,15},{16,17},{18,... | collective-permute-start | bytes 2359304 | tf_op jit(solution)/shard_map/ppermute | solution.py:141
  115.8 21.2 %copy-start.13 = (bf16[512,768]{0,1:T(8,128)(2,1)}, bf16[512,768]{0,1:T(8,128)(2,1)S(1)}, u32[]{:S(2)}) copy-start(bf16[512,768]{0,1:T(8,128)(2,1)S(1)} %copy.102) | copy-start | bytes 2359300
  115.8 58.9 %collective-permute-start.2 = (bf16[512,12,64]{0,2,1:T(8,128)(2,1)S(1)}, bf16[512,12,64]{0,2,1:T(8,128)(2,1)}, u32[]{:S(2)}, u32[]{:S(2)}) collective-permute-start(bf16[512,12,64]{0,2,1:T(8,128)(2,1)S(1)} %bitcast.145), channel_id=1, source_target_pairs={{1,0},{3,2},{5,4},{7,6},{9,8},{11,10},{13,12},{15,14},{17,16},{19,... | collective-permute-start | bytes 2359304 | tf_op jit(solution)/shard_map/ppermute | solution.py:156
  129.2 37.6 %collective-permute-start.1 = (bf16[512,12,64]{0,2,1:T(8,128)(2,1)}, bf16[512,12,64]{0,2,1:T(8,128)(2,1)S(1)}, u32[]{:S(2)}, u32[]{:S(2)}) collective-permute-start(bf16[512,12,64]{0,2,1:T(8,128)(2,1)} %bitcast.160), channel_id=1, source_target_pairs={{0,1},{2,3},{4,5},{6,7},{8,9},{10,11},{12,13},{14,15},{16,17},{18,... | collective-permute-start | bytes 2359304 | tf_op jit(solution)/shard_map/ppermute | solution.py:141
  140.9 26.0 %copy-start.1 = (f32[12,512,512]{1,2,0:T(8,128)}, f32[12,512,512]{1,2,0:T(8,128)S(1)}, u32[]{:S(2)}) copy-start(f32[12,512,512]{1,2,0:T(8,128)S(1)} %get-tuple-element.132) | copy-start | bytes 37748740
  147.0 161.3 %collective-permute-start.3 = (f32[12,512,1]{1,0,2:T(8,128)}, f32[12,512,1]{1,0,2:T(8,128)}, u32[]{:S(2)}, u32[]{:S(2)}) collective-permute-start(f32[12,512,1]{1,0,2:T(8,128)} %bitcast.22), channel_id=1, source_target_pairs={{1,0},{3,2},{5,4},{7,6},{9,8},{11,10},{13,12},{15,14},{17,16},{19,... | collective-permute-start | bytes 73736 | tf_op jit(solution)/shard_map/ppermute | solution.py:156
  152.7 19.6 %copy-start.21 = (bf16[768,768]{0,1:T(8,128)(2,1)S(1)}, bf16[768,768]{0,1:T(8,128)(2,1)}, u32[]{:S(2)}) copy-start(bf16[768,768]{0,1:T(8,128)(2,1)} %reshape.385) | copy-start | bytes 3538948
  244.3 64.1 %collective-permute-start.4 = (bf16[512,12,64]{0,2,1:T(8,128)(2,1)S(1)}, bf16[512,12,64]{0,2,1:T(8,128)(2,1)}, u32[]{:S(2)}, u32[]{:S(2)}) collective-permute-start(bf16[512,12,64]{0,2,1:T(8,128)(2,1)S(1)} %bitcast.151), channel_id=1, source_target_pairs={{1,0},{3,2},{5,4},{7,6},{9,8},{11,10},{13,12},{15,14},{17,16},{19,... | collective-permute-start | bytes 2359304 | tf_op jit(solution)/shard_map/ppermute | solution.py:191
  253.0 160.7 %reduce-scatter.8.cloned.1.call-start = ((), (), s32[]{:S(2)}) async-start(), calls=%async_computation.5 | async-start | bytes 7962624 | tf_op jit(solution)/shard_map/reduce_scatter | solution.py:58
  273.1 11.8 %copy-start.8 = (bf16[512,768]{0,1:T(8,128)(2,1)S(1)}, bf16[512,768]{0,1:T(8,128)(2,1)}, u32[]{:S(2)}) copy-start(bf16[512,768]{0,1:T(8,128)(2,1)} %copy-done.7) | copy-start | bytes 2359300
  283.4 34.2 %collective-permute-start.5 = (f32[12,512,1]{1,0,2:T(8,128)S(1)}, f32[12,512,1]{1,0,2:T(8,128)S(1)}, u32[]{:S(2)}, u32[]{:S(2)}) collective-permute-start(f32[12,512,1]{1,0,2:T(8,128)S(1)} %bitcast.177), channel_id=1, source_target_pairs={{1,0},{3,2},{5,4},{7,6},{9,8},{11,10},{13,12},{15,14},{17,16},{19,... | collective-permute-start | bytes 73736 | tf_op jit(solution)/shard_map/ppermute | solution.py:191
  284.9 15.9 %slice-start = ((s8[12582912]{0:T(1024)(128)(4,1)}), s8[4194304]{0:T(1024)(128)(4,1)S(1)}, s32[]{:S(2)}) async-start(s8[12582912]{0:T(1024)(128)(4,1)} %bitcast.135), calls=%async_computation.12 | async-start | bytes 8388608
  284.9 15.9 %slice-start.1 = ((s8[12582912]{0:T(1024)(128)(4,1)}), s8[4194304]{0:T(1024)(128)(4,1)S(1)}, s32[]{:S(2)}) async-start(s8[12582912]{0:T(1024)(128)(4,1)} %bitcast.135), calls=%async_computation.13 | async-start | bytes 8388608
  286.4 14.4 %slice-start.2 = ((s8[12582912]{0:T(1024)(128)(4,1)}), s8[4194304]{0:T(1024)(128)(4,1)S(1)}, s32[]{:S(2)}) async-start(s8[12582912]{0:T(1024)(128)(4,1)} %bitcast.135), calls=%async_computation.14 | async-start | bytes 8388608
  317.7 12.5 %copy-start.5 = (bf16[512,768]{1,0:T(8,128)(2,1)S(1)}, bf16[512,768]{1,0:T(8,128)(2,1)}, u32[]{:S(2)}) copy-start(bf16[512,768]{1,0:T(8,128)(2,1)} %param.18) | copy-start | bytes 2359300
  317.7 12.6 %copy-start.28 = (f32[768]{0:T(1024)S(1)}, f32[768]{0:T(1024)}, u32[]{:S(2)}) copy-start(f32[768]{0:T(1024)} %copy-done.27) | copy-start | bytes 9220
  317.7 12.6 %copy-start.30 = (f32[512]{0:T(512)S(1)}, f32[512]{0:T(512)}, u32[]{:S(2)}) copy-start(f32[512]{0:T(512)} %copy-done.29) | copy-start | bytes 6148
  317.7 12.6 %copy-start.35 = (f32[512]{0:T(512)S(1)}, f32[512]{0:T(512)}, u32[]{:S(2)}) copy-start(f32[512]{0:T(512)} %copy-done.34) | copy-start | bytes 6148
  317.7 12.5 %copy-start.43 = (f32[768]{0:T(1024)S(1)}, f32[768]{0:T(1024)}, u32[]{:S(2)}) copy-start(f32[768]{0:T(1024)} %copy-done.42) | copy-start | bytes 9220
  337.0 156.9 %reduce-scatter.12.cloned.1.call-start = ((), (), s32[]{:S(2)}) async-start(), calls=%async_computation.7 | async-start | bytes 10616832 | tf_op jit(solution)/shard_map/reduce_scatter | solution.py:58
  337.6 236.5 %reduce-scatter.16.cloned.1.call-start = ((), (), s32[]{:S(2)}) async-start(), calls=%async_computation.11 | async-start | bytes 10616832
  347.4 304.8 %reduce-scatter.14.cloned.1.call-start = ((), (), s32[]{:S(2)}) async-start(), calls=%async_computation.8 | async-start | bytes 4423680 | tf_op jit(solution)/shard_map/reduce_scatter | solution.py:67
  (30 other events, 115.5 us)
Sparse Core Ops, SparseCore 0:
  11.4 66.2 all-gather.4
  81.1 95.8 all-gather.6
  253.1 52.7 reduce-scatter.9
  337.2 76.5 reduce-scatter.7
  417.1 76.8 reduce-scatter.11
  497.3 76.8 reduce-scatter.15
  584.6 67.5 reduce-scatter.13
